TPU v7x, 512 devices: a whole 4x8x8 slice. The times are simulated.
512 devices in a mesh: expert: 128 (over z, y, core), tensor: 4 (over x).
Axes of the slice: x: 4, y: 8, z: 8, core: 2. Of those that a mesh axis runs over, the one named last changes fastest.
Arguments:
- attn_partial: bfloat16 [4, 4096, 3584], P('tensor', 'expert'), may hold values from -4 to 4
- residual_in: bfloat16 [4096, 3584], P(('expert', 'tensor')), may hold values from -6 to 6
- norm_gain: bfloat16 [3584], replicated, may hold values from 0.25 to 1.75
- w_in: bfloat16 [128, 3584, 1024], P('expert', None, 'tensor'), may hold values from -0.09375 to 0.09375
- w_out: bfloat16 [128, 1024, 3584], P('expert', 'tensor'), may hold values from -0.375 to 0.375
- routes: int32 [4096, 8], P('expert'), may hold values from 0 to 127, all different within a row; in each aligned block of 32 rows (0 to 31, 32 to 63, ...) at most 4 rows name the same one
- gate_weights: float32 [4096, 8], P('expert'), may hold values from 0.05 to 0.5
Outputs:
- layer_out: bfloat16 [4096, 3584], P('expert')
Inputs may be any that keep to these rules, and one draw needn't show every extreme that they name: `routes`: each row names 8 different experts. In each aligned block of 32 rows (the tokens of one index of expert) no expert is named by more than 4 rows, and in some block an expert is named by exactly 4 rows.
All inputs are finite; a program needn't handle non-finite values.
Results may differ from a plain program's by a relative error of at most 0.02.
Values may be sent and summed in bfloat16 or wider, within the bound.
No kernel may reach another device: no remote copies, remote signals or barrier semaphores. Data moves between devices by JAX's collectives and lax.ppermute only.
A program may use at most 64 MiB of HBM per device.

v0:
```python
import jax
import jax.numpy as jnp
from jax import lax
from jax.sharding import PartitionSpec as P

QB = 128


EPSILON = 1e-06


def capacity(group_tokens, top_count, expert_count):
    return min(group_tokens, max(4, 2 * group_tokens * top_count // expert_count))


def shards(attn_partial, residual_in, norm_gain, w_in, w_out, routes, gate_weights):
    group_tokens, top_count = routes.shape
    model_width = residual_in.shape[1]
    expert_count = lax.axis_size("expert")
    slot_count = capacity(group_tokens, top_count, expert_count)
    block_count = model_width // QB
    attention = lax.psum_scatter(
        attn_partial[0].astype(jnp.float32).astype(jnp.bfloat16),
        "tensor",
        scatter_dimension=0,
        tiled=True,
    ).astype(jnp.float32)
    residual = (residual_in.astype(jnp.float32) + attention).astype(jnp.bfloat16)
    stream = residual.astype(jnp.float32)
    rms_value = jnp.sqrt(jnp.mean(stream * stream, axis=1, keepdims=True) + EPSILON)
    normed = stream / rms_value * norm_gain.astype(jnp.float32)
    blocks = normed.reshape(-1, block_count, QB)
    block_scale = (jnp.max(jnp.abs(blocks), axis=2) + EPSILON).astype(jnp.bfloat16)
    quantized = (
        (blocks / block_scale.astype(jnp.float32)[:, :, None])
        .astype(jnp.bfloat16)
        .reshape(-1, model_width)
    )
    group_quant, group_scale, group_resid = (
        lax.all_gather(quantized, "tensor", axis=0, tiled=True),
        lax.all_gather(block_scale, "tensor", axis=0, tiled=True),
        lax.all_gather(residual, "tensor", axis=0, tiled=True),
    )
    pair_expert = routes.reshape(-1)
    onehot = (pair_expert[:, None] == jnp.arange(expert_count, dtype=jnp.int32)[None, :]).astype(
        jnp.int32
    )
    earlier = jnp.cumsum(onehot, axis=0) - onehot
    slot_index = jnp.sum(earlier * onehot, axis=1)
    target = pair_expert * slot_count + slot_index
    pair_total = group_tokens * top_count
    slot_table = (
        jnp.full((expert_count * slot_count,), -1, jnp.int32)
        .at[target]
        .set(jnp.arange(pair_total, dtype=jnp.int32))
    )
    slot_table = slot_table.reshape(expert_count, slot_count)
    filled = slot_table >= 0
    token_ids = jnp.maximum(slot_table, 0) // top_count
    row_block = jnp.where(filled[:, :, None], group_quant[token_ids], jnp.zeros((), jnp.bfloat16))
    scales = jnp.where(filled[:, :, None], group_scale[token_ids], jnp.zeros((), jnp.bfloat16))
    recv_rows, recv_scales = (
        lax.all_to_all(row_block, "expert", split_axis=0, concat_axis=0, tiled=True),
        lax.all_to_all(scales, "expert", split_axis=0, concat_axis=0, tiled=True),
    )
    sources = recv_rows.shape[0]
    widened = recv_rows.reshape(sources, slot_count, block_count, QB).astype(jnp.float32)
    expert_input = (
        (widened * recv_scales.astype(jnp.float32)[:, :, :, None])
        .reshape(sources * slot_count, model_width)
        .astype(jnp.bfloat16)
    )
    hidden = jax.nn.silu(jnp.dot(expert_input, w_in[0], preferred_element_type=jnp.float32)).astype(
        jnp.bfloat16
    )
    partial_value = jnp.dot(hidden, w_out[0], preferred_element_type=jnp.float32).reshape(
        sources, slot_count, model_width
    )
    summed = lax.psum_scatter(
        partial_value.astype(jnp.bfloat16), "tensor", scatter_dimension=2, tiled=True
    )
    returned = lax.all_to_all(summed, "expert", split_axis=0, concat_axis=0, tiled=True)
    quarter = returned.shape[2]
    flat_back = returned.reshape(expert_count * slot_count, quarter)
    picked = flat_back[target].astype(jnp.float32) * gate_weights.reshape(-1)[:, None]
    mixture = jnp.sum(picked.reshape(group_tokens, top_count, quarter), axis=1)
    resid_part = lax.dynamic_slice_in_dim(
        group_resid, lax.axis_index("tensor") * quarter, quarter, 1
    )
    out_part = (resid_part.astype(jnp.float32) + mixture).astype(jnp.bfloat16)
    return lax.all_gather(out_part, "tensor", axis=1, tiled=True)


def solution(mesh):
    return jax.shard_map(
        shards,
        mesh=mesh,
        in_specs=(
            P("tensor", "expert", None),
            P(("expert", "tensor"), None),
            P(),
            P("expert", None, "tensor"),
            P("expert", "tensor", None),
            P("expert", None),
            P("expert", None),
        ),
        out_specs=P("expert", None),
        check_vma=False,
    )
```

profile of v0, /device:TPU:8, one launch (start us, length us, event | category | flops | bytes accessed | tf_op | source)
XLA Modules:
  0.0 353.7 jit_solution(2906047092379469535)
XLA Ops:
  6.5 0.7 reduce-scatter.5.cloned.1.call-update
  7.3 0.8 copy.82
  9.7 1.4 scatter_custom_fusion
  12.3 28.5 %reduce-scatter.5.cloned.1.call-done = bf16[8,3584]{1,0:T(8,128)(2,1)} async-done(((bf16[32,3584]{1,0:T(8,128)(2,1)}), bf16[8,3584]{1,0:T(8,128)(2,1)}) %reduce-scatter.5.cloned.1.call-update) | async-done | bytes 57360 | tf_op jit(solution)/shard_map/reduce_scatter | solution.py:22
  40.9 1.0 fusion.16
  42.2 10.4 %all_gather.14 = bf16[32,28]{1,0:T(8,128)(2,1)S(1)} all-gather(bf16[8,28]{1,0:T(8,128)(2,1)S(1)} %add_convert_fusion.2), channel_id=1, replica_groups=mesh['expert'=128,'tensor'=4] {'tensor'}, dimensions={0}, use_global_device_ids=true | all-gather | bytes 2240 | tf_op jit(solution)/shard_map/all_gather | solution.py:41
  52.8 12.2 %all_gather.13 = bf16[32,3584]{1,0:T(8,128)(2,1)S(1)} all-gather(bf16[8,3584]{1,0:T(8,128)(2,1)S(1)} %fusion.18), channel_id=1, replica_groups=mesh['expert'=128,'tensor'=4] {'tensor'}, dimensions={0}, use_global_device_ids=true | all-gather | bytes 286720 | tf_op jit(solution)/shard_map/all_gather | solution.py:40
  65.0 4.2 %gather_fusion = bf16[512,3584]{1,0:T(8,128)(2,1)} fusion(bf16[32,3584]{1,0:T(8,128)(2,1)S(1)} %all_gather.13, s32[1024]{0:T(1024)S(1)} %pad_clamp_fusion.1), kind=kCustom, calls=%fused_computation | custom fusion | bytes 7342080 | tf_op jit(solution)/shard_map/gather | solution.py:60
  69.1 7.0 %reshape.168 = bf16[128,4,3584]{2,1,0:T(4,128)(2,1)} reshape(bf16[512,3584]{1,0:T(8,128)(2,1)} %gather_fusion) | data formatting | bytes 7340032 | tf_op jit(solution)/shard_map/gather | solution.py:60
  76.2 1.3 gather_fusion.1
  77.5 0.9 broadcast_select_fusion.1
  78.4 14.1 %all-to-all-start.1 = ((bf16[128,4,28]{2,1,0:T(4,128)(2,1)}), bf16[128,4,28]{2,1,0:T(4,128)(2,1)S(1)}, u32[]{:S(2)}, u32[]{:S(2)}) async-start(bf16[128,4,28]{2,1,0:T(4,128)(2,1)} %broadcast_select_fusion.1), calls=%async_computation.2 | async-start | bytes 262144 | tf_op jit(solution)/shard_map/all_to_all | solution.py:64
  92.5 5.6 %broadcast_select_fusion = bf16[128,4,3584]{2,1,0:T(4,128)(2,1)} fusion(bf16[128,4,3584]{2,1,0:T(4,128)(2,1)} %reshape.168, pred[128,4]{1,0:T(8,128)(4,1)S(1)} %ge.11), kind=kLoop, calls=%fused_computation.11 | loop fusion | flops 1835008 | bytes 7340544 | tf_op jit(solution)/shard_map/jit(_where)/select_n | solution.py:60
  98.1 6.3 %all-to-all-done.1 = bf16[128,4,28]{2,1,0:T(4,128)(2,1)S(1)} async-done(((bf16[128,4,28]{2,1,0:T(4,128)(2,1)}), bf16[128,4,28]{2,1,0:T(4,128)(2,1)S(1)}, u32[]{:S(2)}, u32[]{:S(2)}) %all-to-all-start.1) | async-done | bytes 28704 | tf_op jit(solution)/shard_map/all_to_all | solution.py:64
  104.4 7.8 %all-to-all-start = ((bf16[128,4,3584]{2,1,0:T(4,128)(2,1)}), bf16[128,4,3584]{2,1,0:T(4,128)(2,1)}, u32[]{:S(2)}, u32[]{:S(2)}) async-start(bf16[128,4,3584]{2,1,0:T(4,128)(2,1)} %broadcast_select_fusion), calls=%async_computation.1 | async-start | bytes 7340032 | tf_op jit(solution)/shard_map/all_to_all | solution.py:63
  112.7 86.9 %all-to-all-done = bf16[128,4,3584]{2,1,0:T(4,128)(2,1)} async-done(((bf16[128,4,3584]{2,1,0:T(4,128)(2,1)}), bf16[128,4,3584]{2,1,0:T(4,128)(2,1)}, u32[]{:S(2)}, u32[]{:S(2)}) %all-to-all-start) | async-done | bytes 3670048 | tf_op jit(solution)/shard_map/all_to_all | solution.py:63
  199.6 7.2 %copy.88 = bf16[128,4,3584]{0,2,1:T(8,128)(2,1)} copy(bf16[128,4,3584]{2,1,0:T(4,128)(2,1)} %all-to-all-done) | data formatting | bytes 7340032 | tf_op jit(solution)/shard_map/all_to_all | solution.py:63
  206.8 5.5 %fusion = bf16[128,4,28,128]{0,3,2,1:T(8,128)(2,1)} fusion(bf16[128,4,28,128]{0,3,2,1:T(8,128)(2,1)} %bitcast.54, f32[128,4,28]{0,2,1:T(8,128)S(1)} %copy.90), kind=kLoop, calls=%fused_computation.5 | loop fusion | flops 5505024 | bytes 7397376 | tf_op jit(solution)/shard_map/convert_element_type | solution.py:71
  212.3 7.8 %copy.91 = bf16[128,4,28,128]{3,2,1,0:T(8,128)(2,1)} copy(bf16[128,4,28,128]{0,3,2,1:T(8,128)(2,1)} %fusion) | data formatting | bytes 7340032 | tf_op jit(solution)/shard_map/convert_element_type | solution.py:71
  220.2 4.0 %multiply_convert_fusion = bf16[512,256]{1,0:T(8,128)(2,1)S(1)} fusion(bf16[1,3584,256]{2,1,0:T(8,128)(2,1)} %param.10, bf16[64,8,28,128]{3,2,1,0:T(8,128)(2,1)} %bitcast.56), kind=kOutput, calls=%fused_computation.16 | convolution fusion | flops 940179456 | bytes 5767168 | tf_op jit(solution)/shard_map/dot_general | solution.py:73
  224.3 3.0 convolution_convert_fusion
  227.2 6.8 %copy.95 = bf16[128,4,3584]{0,1,2:T(4,128)(2,1)} copy(bf16[128,4,3584]{2,0,1:T(8,128)(2,1)} %convolution_convert_fusion) | data formatting | bytes 7340032
  234.0 4.5 %copy.109 = bf16[448,8,4,128]{3,1,2,0:T(8,128)(2,1)} copy(bf16[448,8,4,128]{3,2,1,0:T(4,128)(2,1)} %bitcast.55) | data formatting | bytes 7340032
  238.6 44.7 %reduce-scatter.7.cloned.1.call-done = bf16[896,512]{1,0:T(8,128)(2,1)} async-done(((bf16[3584,512]{1,0:T(8,128)(2,1)}), bf16[896,512]{1,0:T(8,128)(2,1)}) %reduce-scatter.7.cloned.1.call-update) | async-done | bytes 917520
  283.3 1.9 reshape.203
  285.2 2.3 copy.93
  287.5 14.6 %all-to-all-start.2 = ((bf16[128,4,896]{2,1,0:T(4,128)(2,1)}), bf16[128,4,896]{2,1,0:T(4,128)(2,1)}, u32[]{:S(2)}, u32[]{:S(2)}) async-start(bf16[128,4,896]{2,1,0:T(4,128)(2,1)} %copy.93), calls=%async_computation.3 | async-start | bytes 1835008 | tf_op jit(solution)/shard_map/all_to_all | solution.py:82
  302.2 12.2 %all_gather.12 = bf16[32,3584]{1,0:T(8,128)(2,1)S(1)} all-gather(bf16[8,3584]{1,0:T(8,128)(2,1)S(1)} %get-tuple-element.6), channel_id=1, replica_groups=mesh['expert'=128,'tensor'=4] {'tensor'}, dimensions={0}, use_global_device_ids=true | all-gather | bytes 286720 | tf_op jit(solution)/shard_map/all_gather | solution.py:42
  314.4 16.0 %all-to-all-done.2 = bf16[128,4,896]{2,1,0:T(4,128)(2,1)} async-done(((bf16[128,4,896]{2,1,0:T(4,128)(2,1)}), bf16[128,4,896]{2,1,0:T(4,128)(2,1)}, u32[]{:S(2)}, u32[]{:S(2)}) %all-to-all-start.2) | async-done | bytes 917536 | tf_op jit(solution)/shard_map/all_to_all | solution.py:82
  330.3 1.6 reshape.164
  332.0 1.2 gather_fusion.2
  333.6 12.6 %all_gather.15 = bf16[32,3584]{1,0:T(8,128)(2,1)S(1)} all-gather(bf16[32,896]{1,0:T(8,128)(2,1)S(1)} %add_convert_fusion), channel_id=1, replica_groups=mesh['expert'=128,'tensor'=4] {'tensor'}, dimensions={1}, use_global_device_ids=true | all-gather | bytes 286720 | tf_op jit(solution)/shard_map/all_gather | solution.py:91
  (46 shorter events, 4.9 us)
Async XLA Ops:
  6.5 217.7 %copy-start = (bf16[1,256,3584]{2,1,0:T(8,128)(2,1)S(1)}, bf16[1,256,3584]{2,1,0:T(8,128)(2,1)}, u32[]{:S(2)}) copy-start(bf16[1,256,3584]{2,1,0:T(8,128)(2,1)} %param.11) | copy-start | bytes 5505028
  6.5 34.3 %reduce-scatter.5.cloned.1.call-start = ((), (), s32[]{:S(2)}) async-start(), calls=%async_computation.5 | async-start | bytes 286720 | tf_op jit(solution)/shard_map/reduce_scatter | solution.py:22
  78.4 26.1 %all-to-all-start.1 = ((bf16[128,4,28]{2,1,0:T(4,128)(2,1)}), bf16[128,4,28]{2,1,0:T(4,128)(2,1)S(1)}, u32[]{:S(2)}, u32[]{:S(2)}) async-start(bf16[128,4,28]{2,1,0:T(4,128)(2,1)} %broadcast_select_fusion.1), calls=%async_computation.2 | async-start | bytes 262144 | tf_op jit(solution)/shard_map/all_to_all | solution.py:64
  104.4 95.1 %all-to-all-start = ((bf16[128,4,3584]{2,1,0:T(4,128)(2,1)}), bf16[128,4,3584]{2,1,0:T(4,128)(2,1)}, u32[]{:S(2)}, u32[]{:S(2)}) async-start(bf16[128,4,3584]{2,1,0:T(4,128)(2,1)} %broadcast_select_fusion), calls=%async_computation.1 | async-start | bytes 7340032 | tf_op jit(solution)/shard_map/all_to_all | solution.py:63
  112.3 171.0 %reduce-scatter.7.cloned.1.call-start = ((), (), s32[]{:S(2)}) async-start(), calls=%async_computation.6 | async-start | bytes 4587520
  238.6 63.5 %copy-start.1 = (f32[32,8]{0,1:T(8,128)S(1)}, f32[32,8]{0,1:T(8,128)}, u32[]{:S(2)}) copy-start(f32[32,8]{0,1:T(8,128)} %param.13) | copy-start | bytes 3076
  287.5 42.8 %all-to-all-start.2 = ((bf16[128,4,896]{2,1,0:T(4,128)(2,1)}), bf16[128,4,896]{2,1,0:T(4,128)(2,1)}, u32[]{:S(2)}, u32[]{:S(2)}) async-start(bf16[128,4,896]{2,1,0:T(4,128)(2,1)} %copy.93), calls=%async_computation.3 | async-start | bytes 1835008 | tf_op jit(solution)/shard_map/all_to_all | solution.py:82
Sparse Core Ops, SparseCore 0:
  10.1 30.6 reduce-scatter.4
  238.7 44.5 reduce-scatter.6
where the time goes:
time: 355 us; the launch traced here: 354 us
  waiting for transfers between devices  183 us (52%)
  local copies, waits for them, and re-layouts  50.2 us (14%)
  blocking collectives  47.4 us (13%)
  starting transfers between devices  36.8 us (10%)
  other arithmetic  15.5 us (4%)
  between operations  13.6 us (4%)
  matrix products  6.96 us (2%)
    all_to_all x1, waiting for transfers between devices, shards(): lax.all_to_all(row_block, 'expert', split_axis=0, concat_axis=0, tiled=True)  86.9 us
    unnamed x3, waiting for transfers between devices  45.5 us
    reduce_scatter x1, waiting for transfers between devices, shards(): lax.psum_scatter(attn_partial[0].astype(jnp.float32).astype(jnp.bfloat16)...  28.5 us
    all_to_all x1, waiting for transfers between devices, shards(): lax.all_to_all(summed, 'expert', split_axis=0, concat_axis=0, tiled=True)  16 us
    unnamed x11, local copies, waits for them, and re-layouts  14.7 us
    all_to_all x1, starting transfers between devices, shards(): lax.all_to_all(summed, 'expert', split_axis=0, concat_axis=0, tiled=True)  14.6 us
    all_to_all x1, starting transfers between devices, shards(): lax.all_to_all(scales, 'expert', split_axis=0, concat_axis=0, tiled=True)  14.1 us
    all_gather x1, blocking collectives, shards(): return lax.all_gather(out_part, 'tensor', axis=1, tiled=True)  12.6 us
  transfers between devices with their start and end apart: 5, of which 5 were waited for; matrix products, arithmetic and copies ran while one was open for 3% of the time, Pallas kernels for 0%

commit v1 on v0

v1 whole, which is shorter than its diff:
```python
import jax
import jax.numpy as jnp
from jax import lax
from jax.sharding import PartitionSpec as P

QB = 128


EPSILON = 1e-06


def capacity(group_tokens, top_count, expert_count):
    return min(group_tokens, max(4, 2 * group_tokens * top_count // expert_count))


def shards(attn_partial, residual_in, norm_gain, w_in, w_out, routes, gate_weights):
    group_tokens, top_count = routes.shape
    model_width = residual_in.shape[1]
    expert_count = lax.axis_size("expert")
    tensor_count = lax.axis_size("tensor")
    slot_count = capacity(group_tokens, top_count, expert_count)
    block_count = model_width // QB
    w_in_d = lax.all_to_all(w_in[0], "tensor", split_axis=0, concat_axis=1, tiled=True)
    w_out_d = lax.all_to_all(w_out[0], "tensor", split_axis=1, concat_axis=0, tiled=True)
    hidden_count = w_in_d.shape[1]
    hidden_quarter = hidden_count // tensor_count
    attention = lax.psum_scatter(
        attn_partial[0].astype(jnp.float32).astype(jnp.bfloat16),
        "tensor",
        scatter_dimension=0,
        tiled=True,
    ).astype(jnp.float32)
    residual = (residual_in.astype(jnp.float32) + attention).astype(jnp.bfloat16)
    stream = residual.astype(jnp.float32)
    rms_value = jnp.sqrt(jnp.mean(stream * stream, axis=1, keepdims=True) + EPSILON)
    normed = stream / rms_value * norm_gain.astype(jnp.float32)
    blocks = normed.reshape(-1, block_count, QB)
    block_scale = (jnp.max(jnp.abs(blocks), axis=2) + EPSILON).astype(jnp.bfloat16)
    scale_wide = block_scale.astype(jnp.float32)[:, :, None]
    quantized = (blocks / scale_wide).astype(jnp.bfloat16)
    expert_input = (
        (quantized.astype(jnp.float32) * scale_wide).reshape(-1, model_width).astype(jnp.bfloat16)
    )
    both = lax.all_to_all(
        jnp.stack([expert_input, residual]), "tensor", split_axis=2, concat_axis=1, tiled=True
    )
    group_input, group_resid = both[0], both[1]
    pair_expert = routes.reshape(-1)
    onehot = (pair_expert[:, None] == jnp.arange(expert_count, dtype=jnp.int32)[None, :]).astype(
        jnp.int32
    )
    earlier = jnp.cumsum(onehot, axis=0) - onehot
    slot_index = jnp.sum(earlier * onehot, axis=1)
    target = pair_expert * slot_count + slot_index
    pair_total = group_tokens * top_count
    slot_table = (
        jnp.full((expert_count * slot_count,), -1, jnp.int32)
        .at[target]
        .set(jnp.arange(pair_total, dtype=jnp.int32))
    )
    slot_table = slot_table.reshape(expert_count, slot_count)
    filled = slot_table >= 0
    token_ids = jnp.maximum(slot_table, 0) // top_count
    row_block = jnp.where(filled[:, :, None], group_input[token_ids], jnp.zeros((), jnp.bfloat16))
    recv_rows = lax.all_to_all(row_block, "expert", split_axis=0, concat_axis=0, tiled=True)
    sources = recv_rows.shape[0]
    quarter = recv_rows.shape[2]
    rows = recv_rows.reshape(sources * slot_count, quarter)
    pre_partial = jnp.dot(rows, w_in_d, preferred_element_type=jnp.float32)
    pre_value = lax.psum_scatter(pre_partial, "tensor", scatter_dimension=1, tiled=True)
    hidden_part = jax.nn.silu(pre_value).astype(jnp.bfloat16)
    hidden = lax.all_gather(hidden_part, "tensor", axis=1, tiled=True)
    summed = jnp.zeros((rows.shape[0], quarter), jnp.float32)
    for lane in range(tensor_count):
        lo = lane * hidden_quarter
        term = jnp.dot(
            hidden[:, lo : lo + hidden_quarter],
            w_out_d[lo : lo + hidden_quarter],
            preferred_element_type=jnp.float32,
        ).astype(jnp.bfloat16)
        summed = summed + term.astype(jnp.float32)
    expert_out = summed.astype(jnp.bfloat16).reshape(sources, slot_count, quarter)
    returned = lax.all_to_all(expert_out, "expert", split_axis=0, concat_axis=0, tiled=True)
    flat_back = returned.reshape(expert_count * slot_count, quarter)
    picked = flat_back[target].astype(jnp.float32) * gate_weights.reshape(-1)[:, None]
    mixture = jnp.sum(picked.reshape(group_tokens, top_count, quarter), axis=1)
    out_part = (group_resid.astype(jnp.float32) + mixture).astype(jnp.bfloat16)
    return lax.all_gather(out_part, "tensor", axis=1, tiled=True)


def solution(mesh):
    return jax.shard_map(
        shards,
        mesh=mesh,
        in_specs=(
            P("tensor", "expert", None),
            P(("expert", "tensor"), None),
            P(),
            P("expert", None, "tensor"),
            P("expert", "tensor", None),
            P("expert", None),
            P("expert", None),
        ),
        out_specs=P("expert", None),
        check_vma=False,
    )
```

time: 355 us -> 266 us (0.75)
  the two profiles are of different devices: /device:TPU:8 before, /device:TPU:10 now
where the time goes in v1:
time: 266 us; the launch traced here: 265 us
  waiting for transfers between devices  122 us (46%)
  blocking collectives  45.5 us (17%)
  starting transfers between devices  39.3 us (15%)
  local copies, waits for them, and re-layouts  29.7 us (11%)
  between operations  13.4 us (5%)
  matrix products  7.82 us (3%)
  other arithmetic  6.91 us (3%)
    all_to_all x1, blocking collectives, shards(): lax.all_to_all(w_out[0], 'tensor', split_axis=1, concat_axis=0, tiled=True)  33.2 us
    reduce_scatter x1, waiting for transfers between devices, shards(): lax.psum_scatter(attn_partial[0].astype(jnp.float32).astype(jnp.bfloat16)...  28.8 us
    all_to_all x1, waiting for transfers between devices, shards(): lax.all_to_all(expert_out, 'expert', split_axis=0, concat_axis=0, tiled=T...  28.5 us
    all_to_all x1, waiting for transfers between devices, shards(): lax.all_to_all(row_block, 'expert', split_axis=0, concat_axis=0, tiled=True)  26.1 us
    reduce_scatter x1, waiting for transfers between devices, shards(): lax.psum_scatter(pre_partial, 'tensor', scatter_dimension=1, tiled=True)  25.9 us
    all_to_all x1, starting transfers between devices, shards(): lax.all_to_all(row_block, 'expert', split_axis=0, concat_axis=0, tiled=True)  14.2 us
    all_to_all x1, starting transfers between devices, shards(): lax.all_to_all(expert_out, 'expert', split_axis=0, concat_axis=0, tiled=T...  14.2 us
    all_gather x1, blocking collectives, shards(): return lax.all_gather(out_part, 'tensor', axis=1, tiled=True)  12.2 us
  transfers between devices with their start and end apart: 7, of which 7 were waited for; matrix products, arithmetic and copies ran while one was open for 9% of the time, Pallas kernels for 0%

profile of v1, /device:TPU:10, one launch (start us, length us, event | category | flops | bytes accessed | tf_op | source)
XLA Modules:
  0.0 264.9 jit_solution(16002327998737600328)
XLA Ops:
  7.3 0.8 copy.47
  10.2 28.8 %reduce-scatter.3.cloned.1.call-done = bf16[8,3584]{1,0:T(8,128)(2,1)} async-done(((bf16[32,3584]{1,0:T(8,128)(2,1)}), bf16[8,3584]{1,0:T(8,128)(2,1)}) %reduce-scatter.3.cloned.1.call-update) | async-done | bytes 57360 | tf_op jit(solution)/shard_map/reduce_scatter | solution.py:27
  39.0 1.0 fusion.9
  40.3 2.5 copy.44
  42.8 2.6 reshape.198
  45.4 5.7 %all-to-all-start = ((bf16[4,2,7168]{2,1,0:T(2,128)(2,1)}), bf16[4,2,7168]{2,1,0:T(2,128)(2,1)S(1)}, u32[]{:S(2)}, u32[]{:S(2)}) async-start(bf16[4,2,7168]{2,1,0:T(2,128)(2,1)} %reshape.198), calls=%async_computation.1 | async-start | bytes 229376 | tf_op jit(solution)/shard_map/all_to_all | solution.py:44
  51.3 4.3 %all-to-all-done = bf16[4,2,7168]{2,1,0:T(2,128)(2,1)S(1)} async-done(((bf16[4,2,7168]{2,1,0:T(2,128)(2,1)}), bf16[4,2,7168]{2,1,0:T(2,128)(2,1)S(1)}, u32[]{:S(2)}, u32[]{:S(2)}) %all-to-all-start) | async-done | bytes 114720 | tf_op jit(solution)/shard_map/all_to_all | solution.py:44
  55.6 5.0 %all-to-all-start.2 = ((bf16[4,896,256]{2,1,0:T(8,128)(2,1)}), bf16[4,896,256]{2,1,0:T(8,128)(2,1)S(1)}, u32[]{:S(2)}, u32[]{:S(2)}) async-start(bf16[4,896,256]{2,1,0:T(8,128)(2,1)} %bitcast.79), calls=%async_computation.3 | async-start | bytes 3670016 | tf_op jit(solution)/shard_map/all_to_all | solution.py:23
  60.6 1.4 scatter_custom_fusion
  62.5 3.4 %reshape.199 = bf16[3584,2,8]{2,1,0:T(2,128)(2,1)} reshape(bf16[4,2,7168]{2,1,0:T(2,128)(2,1)S(1)} %all-to-all-done) | data formatting | bytes 229376
  65.9 4.3 %copy.45 = bf16[2,8,4,896]{3,1,2,0:T(8,128)(2,1)S(1)} copy(bf16[2,8,4,896]{1,0,3,2:T(2,128)(2,1)} %bitcast.78) | data formatting | bytes 229376 | tf_op jit(solution)/shard_map/all_to_all | solution.py:44
  70.3 2.8 %gather_fusion = bf16[512,896]{1,0:T(8,128)(2,1)} fusion(bf16[32,896]{1,0:T(8,128)(2,1)S(1)} %slice_bitcast_fusion.8, s32[1024]{0:T(1024)S(1)} %pad_clamp_fusion.1), kind=kCustom, calls=%fused_computation | custom fusion | bytes 1837056 | tf_op jit(solution)/shard_map/gather | solution.py:64
  73.0 1.8 reshape.172
  74.8 1.5 broadcast_select_fusion
  76.3 3.2 %all-to-all-done.2 = bf16[4,896,256]{2,1,0:T(8,128)(2,1)S(1)} async-done(((bf16[4,896,256]{2,1,0:T(8,128)(2,1)}), bf16[4,896,256]{2,1,0:T(8,128)(2,1)S(1)}, u32[]{:S(2)}, u32[]{:S(2)}) %all-to-all-start.2) | async-done | bytes 1835040 | tf_op jit(solution)/shard_map/all_to_all | solution.py:23
  79.5 14.2 %all-to-all-start.1 = ((bf16[128,4,896]{2,1,0:T(4,128)(2,1)}), bf16[128,4,896]{2,1,0:T(4,128)(2,1)S(1)}, u32[]{:S(2)}, u32[]{:S(2)}) async-start(bf16[128,4,896]{2,1,0:T(4,128)(2,1)} %broadcast_select_fusion), calls=%async_computation.2 | async-start | bytes 1835008 | tf_op jit(solution)/shard_map/all_to_all | solution.py:65
  93.7 2.4 copy.51
  96.2 26.1 %all-to-all-done.1 = bf16[128,4,896]{2,1,0:T(4,128)(2,1)S(1)} async-done(((bf16[128,4,896]{2,1,0:T(4,128)(2,1)}), bf16[128,4,896]{2,1,0:T(4,128)(2,1)S(1)}, u32[]{:S(2)}, u32[]{:S(2)}) %all-to-all-start.1) | async-done | bytes 917536 | tf_op jit(solution)/shard_map/all_to_all | solution.py:65
  122.2 1.1 reshape.166
  123.4 3.8 %fusion.20 = f32[512,1024]{1,0:T(8,128)} fusion(bf16[512,896]{1,0:T(8,128)(2,1)} %reshape.166, bf16[896,1024]{0,1:T(8,128)(2,1)S(1)} %bitcast.80), kind=kOutput, calls=%fused_computation.62 | convolution fusion | flops 939524096 | bytes 4849664 | tf_op jit(solution)/shard_map/dot_general | solution.py:69
  127.4 25.9 %reduce-scatter.5.cloned.1.call-done = f32[512,256]{1,0:T(8,128)} async-done(((f32[512,1024]{1,0:T(8,128)}), f32[512,256]{1,0:T(8,128)}) %reduce-scatter.5.cloned.1.call-update) | async-done | bytes 524304 | tf_op jit(solution)/shard_map/reduce_scatter | solution.py:70
  153.3 1.9 multiply_convert_fusion
  155.3 2.3 copy.52
  157.6 33.2 %all_to_all.60 = bf16[256,4,896]{0,2,1:T(8,128)(2,1)S(1)} all-to-all(bf16[256,4,896]{0,2,1:T(8,128)(2,1)} %bitcast.76), channel_id=1, replica_groups=mesh['expert'=128,'tensor'=4] {'tensor'}, dimensions={1} | all-to-all | bytes 3670016 | tf_op jit(solution)/shard_map/all_to_all | solution.py:24
  190.8 5.0 %all-gather.2.cloned.1.call-done = bf16[512,1024]{1,0:T(8,128)(2,1)} async-done(((bf16[512,256]{1,0:T(8,128)(2,1)}), bf16[512,1024]{1,0:T(8,128)(2,1)}) %all-gather.2.cloned.1.call-update) | async-done | bytes 1048592 | tf_op jit(solution)/shard_map/all_gather | solution.py:72
  195.8 1.5 convolution_convert_fusion.2
  197.3 1.4 convolution_convert_fusion.1
  199.8 1.1 reshape.167
  201.0 14.2 %all-to-all-start.4 = ((bf16[128,4,896]{2,1,0:T(4,128)(2,1)}), bf16[128,4,896]{2,1,0:T(4,128)(2,1)S(1)}, u32[]{:S(2)}, u32[]{:S(2)}) async-start(bf16[128,4,896]{2,1,0:T(4,128)(2,1)} %reshape.167), calls=%async_computation.6 | async-start | bytes 1835008 | tf_op jit(solution)/shard_map/all_to_all | solution.py:83
  215.2 28.5 %all-to-all-done.4 = bf16[128,4,896]{2,1,0:T(4,128)(2,1)S(1)} async-done(((bf16[128,4,896]{2,1,0:T(4,128)(2,1)}), bf16[128,4,896]{2,1,0:T(4,128)(2,1)S(1)}, u32[]{:S(2)}, u32[]{:S(2)}) %all-to-all-start.4) | async-done | bytes 917536 | tf_op jit(solution)/shard_map/all_to_all | solution.py:83
  243.9 1.2 gather_fusion.1
  245.5 12.2 %all_gather.7 = bf16[32,3584]{1,0:T(8,128)(2,1)S(1)} all-gather(bf16[32,896]{1,0:T(8,128)(2,1)S(1)} %fusion.13), channel_id=1, replica_groups=mesh['expert'=128,'tensor'=4] {'tensor'}, dimensions={1}, use_global_device_ids=true | all-gather | bytes 286720 | tf_op jit(solution)/shard_map/all_gather | solution.py:88
  (53 shorter events, 6.6 us)
Async XLA Ops:
  6.5 32.4 %reduce-scatter.3.cloned.1.call-start = ((), (), s32[]{:S(2)}) async-start(), calls=%async_computation.7 | async-start | bytes 286720 | tf_op jit(solution)/shard_map/reduce_scatter | solution.py:27
  45.4 10.1 %all-to-all-start = ((bf16[4,2,7168]{2,1,0:T(2,128)(2,1)}), bf16[4,2,7168]{2,1,0:T(2,128)(2,1)S(1)}, u32[]{:S(2)}, u32[]{:S(2)}) async-start(bf16[4,2,7168]{2,1,0:T(2,128)(2,1)} %reshape.198), calls=%async_computation.1 | async-start | bytes 229376 | tf_op jit(solution)/shard_map/all_to_all | solution.py:44
  55.6 23.9 %all-to-all-start.2 = ((bf16[4,896,256]{2,1,0:T(8,128)(2,1)}), bf16[4,896,256]{2,1,0:T(8,128)(2,1)S(1)}, u32[]{:S(2)}, u32[]{:S(2)}) async-start(bf16[4,896,256]{2,1,0:T(8,128)(2,1)} %bitcast.79), calls=%async_computation.3 | async-start | bytes 3670016 | tf_op jit(solution)/shard_map/all_to_all | solution.py:23
  79.5 42.7 %all-to-all-start.1 = ((bf16[128,4,896]{2,1,0:T(4,128)(2,1)}), bf16[128,4,896]{2,1,0:T(4,128)(2,1)S(1)}, u32[]{:S(2)}, u32[]{:S(2)}) async-start(bf16[128,4,896]{2,1,0:T(4,128)(2,1)} %broadcast_select_fusion), calls=%async_computation.2 | async-start | bytes 1835008 | tf_op jit(solution)/shard_map/all_to_all | solution.py:65
  93.7 59.7 %reduce-scatter.5.cloned.1.call-start = ((), (), s32[]{:S(2)}) async-start(), calls=%async_computation.8 | async-start | bytes 2621440 | tf_op jit(solution)/shard_map/reduce_scatter | solution.py:70
  96.2 27.2 %copy-start.1 = (bf16[896,4,256]{0,2,1:T(8,128)(2,1)S(1)}, bf16[896,4,256]{0,2,1:T(8,128)(2,1)}, u32[]{:S(2)}) copy-start(bf16[896,4,256]{0,2,1:T(8,128)(2,1)} %copy.51) | copy-start | bytes 5505028
  127.2 28.1 %copy-start = (bf16[1,256,3584]{2,1,0:T(8,128)(2,1)S(1)}, bf16[1,256,3584]{2,1,0:T(8,128)(2,1)}, u32[]{:S(2)}) copy-start(bf16[1,256,3584]{2,1,0:T(8,128)(2,1)} %param.11) | copy-start | bytes 5505028
  127.2 68.6 %all-gather.2.cloned.1.call-start = ((), (), s32[]{:S(2)}) async-start(), calls=%async_computation.9 | async-start | bytes 1310720 | tf_op jit(solution)/shard_map/all_gather | solution.py:72
  195.8 2.9 %copy-start.2 = (bf16[512,1024]{1,0:T(8,128)(2,1)S(1)}, bf16[512,1024]{1,0:T(8,128)(2,1)}, u32[]{:S(2)}) copy-start(bf16[512,1024]{1,0:T(8,128)(2,1)} %all-gather.2.cloned.1.call-done) | copy-start | bytes 3145732
  199.8 15.3 %copy-start.3 = (f32[32,8]{0,1:T(8,128)S(1)}, f32[32,8]{0,1:T(8,128)}, u32[]{:S(2)}) copy-start(f32[32,8]{0,1:T(8,128)} %param.13) | copy-start | bytes 3076
  201.0 42.7 %all-to-all-start.4 = ((bf16[128,4,896]{2,1,0:T(4,128)(2,1)}), bf16[128,4,896]{2,1,0:T(4,128)(2,1)S(1)}, u32[]{:S(2)}, u32[]{:S(2)}) async-start(bf16[128,4,896]{2,1,0:T(4,128)(2,1)} %reshape.167), calls=%async_computation.6 | async-start | bytes 1835008 | tf_op jit(solution)/shard_map/all_to_all | solution.py:83
Sparse Core Ops, SparseCore 0:
  10.1 28.8 reduce-scatter.2
  127.3 25.9 reduce-scatter.4
  155.4 40.2 all-gather.1

commit v2 on v1

--- a/solution.py
+++ b/solution.py
@@ -13,23 +13,31 @@
     return min(group_tokens, max(4, 2 * group_tokens * top_count // expert_count))
 
 
-def shards(attn_partial, residual_in, norm_gain, w_in, w_out, routes, gate_weights):
+def layer(attn_partial, residual_in, norm_gain, w_in, w_out, routes, gate_weights):
     group_tokens, top_count = routes.shape
     model_width = residual_in.shape[1]
     expert_count = lax.axis_size("expert")
     tensor_count = lax.axis_size("tensor")
     slot_count = capacity(group_tokens, top_count, expert_count)
     block_count = model_width // QB
-    w_in_d = lax.all_to_all(w_in[0], "tensor", split_axis=0, concat_axis=1, tiled=True)
-    w_out_d = lax.all_to_all(w_out[0], "tensor", split_axis=1, concat_axis=0, tiled=True)
-    hidden_count = w_in_d.shape[1]
-    hidden_quarter = hidden_count // tensor_count
-    attention = lax.psum_scatter(
-        attn_partial[0].astype(jnp.float32).astype(jnp.bfloat16),
-        "tensor",
-        scatter_dimension=0,
-        tiled=True,
-    ).astype(jnp.float32)
+    w_stack = jnp.stack([w_in[0], w_out[0].T])
+    hidden_quarter = w_stack.shape[2]
+    width_quarter = model_width // tensor_count
+    own = lax.axis_index("tensor")
+    pieces = [lax.dynamic_slice_in_dim(w_stack, own * width_quarter, width_quarter, axis=1)]
+    for shift in range(1, tensor_count):
+        chunk = lax.dynamic_slice_in_dim(
+            w_stack, ((own + shift) % tensor_count) * width_quarter, width_quarter, axis=1
+        )
+        ring = [(u, (u + shift) % tensor_count) for u in range(tensor_count)]
+        pieces.append(lax.ppermute(chunk, "tensor", ring))
+    by_shift = jnp.stack(pieces)
+    w_blocks = by_shift[(own - jnp.arange(tensor_count)) % tensor_count]
+    w_in_d = jnp.concatenate([w_blocks[j, 0] for j in range(tensor_count)], axis=1)
+    head_terms = lax.all_to_all(
+        attn_partial[0].reshape(tensor_count, -1, model_width), "tensor", split_axis=0, concat_axis=0
+    )
+    attention = jnp.sum(head_terms.astype(jnp.float32), axis=0)
     residual = (residual_in.astype(jnp.float32) + attention).astype(jnp.bfloat16)
     stream = residual.astype(jnp.float32)
     rms_value = jnp.sqrt(jnp.mean(stream * stream, axis=1, keepdims=True) + EPSILON)
@@ -41,9 +49,8 @@
     expert_input = (
         (quantized.astype(jnp.float32) * scale_wide).reshape(-1, model_width).astype(jnp.bfloat16)
     )
-    both = lax.all_to_all(
-        jnp.stack([expert_input, residual]), "tensor", split_axis=2, concat_axis=1, tiled=True
-    )
+    both_rows = jnp.stack([expert_input, residual])
+    both = lax.all_to_all(both_rows, "tensor", split_axis=2, concat_axis=1, tiled=True)
     group_input, group_resid = both[0], both[1]
     pair_expert = routes.reshape(-1)
     onehot = (pair_expert[:, None] == jnp.arange(expert_count, dtype=jnp.int32)[None, :]).astype(
@@ -67,15 +74,18 @@
     quarter = recv_rows.shape[2]
     rows = recv_rows.reshape(sources * slot_count, quarter)
     pre_partial = jnp.dot(rows, w_in_d, preferred_element_type=jnp.float32)
-    pre_value = lax.psum_scatter(pre_partial, "tensor", scatter_dimension=1, tiled=True)
+    pre_value = lax.psum_scatter(
+        pre_partial.astype(jnp.bfloat16), "tensor", scatter_dimension=1, tiled=True
+    ).astype(jnp.float32)
     hidden_part = jax.nn.silu(pre_value).astype(jnp.bfloat16)
     hidden = lax.all_gather(hidden_part, "tensor", axis=1, tiled=True)
     summed = jnp.zeros((rows.shape[0], quarter), jnp.float32)
     for lane in range(tensor_count):
         lo = lane * hidden_quarter
-        term = jnp.dot(
+        term = lax.dot_general(
             hidden[:, lo : lo + hidden_quarter],
-            w_out_d[lo : lo + hidden_quarter],
+            w_blocks[lane, 1],
+            (((1,), (1,)), ((), ())),
             preferred_element_type=jnp.float32,
         ).astype(jnp.bfloat16)
         summed = summed + term.astype(jnp.float32)
@@ -90,7 +100,7 @@
 
 def solution(mesh):
     return jax.shard_map(
-        shards,
+        layer,
         mesh=mesh,
         in_specs=(
             P("tensor", "expert", None),

time: 266 us -> 258 us (0.970)
  the two profiles are of different devices: /device:TPU:10 before, /device:TPU:8 now
where the time goes in v2:
time: 258 us; the launch traced here: 257 us
  waiting for transfers between devices  135 us (52%)
  starting transfers between devices  48.7 us (19%)
  local copies, waits for them, and re-layouts  27.2 us (11%)
  between operations  13.8 us (5%)
  blocking collectives  12.2 us (5%)
  other arithmetic  10.9 us (4%)
  matrix products  9.58 us (4%)
    ppermute x3, waiting for transfers between devices, layer(): pieces.append(lax.ppermute(chunk, 'tensor', ring))  38.2 us
    all_gather x1, waiting for transfers between devices, layer(): hidden = lax.all_gather(hidden_part, 'tensor', axis=1, tiled=True)  30.8 us
    reduce_scatter x1, waiting for transfers between devices, layer(): lax.psum_scatter(pre_partial.astype(jnp.bfloat16), 'tensor', scatter_dime...  29.7 us
    all_to_all x1, waiting for transfers between devices, layer(): lax.all_to_all(expert_out, 'expert', split_axis=0, concat_axis=0, tiled=T...  28.5 us
    all_to_all x1, starting transfers between devices, layer(): lax.all_to_all(row_block, 'expert', split_axis=0, concat_axis=0, tiled=True)  17.4 us
    all_to_all x1, starting transfers between devices, layer(): lax.all_to_all(expert_out, 'expert', split_axis=0, concat_axis=0, tiled=T...  14.2 us
    all_gather x1, blocking collectives, layer(): return lax.all_gather(out_part, 'tensor', axis=1, tiled=True)  12.2 us
    ppermute x3, starting transfers between devices, layer(): pieces.append(lax.ppermute(chunk, 'tensor', ring))  9.4 us
  transfers between devices with their start and end apart: 9, of which 7 were waited for; matrix products, arithmetic and copies ran while one was open for 7% of the time, Pallas kernels for 0%

profile of v2, /device:TPU:8, one launch (start us, length us, event | category | flops | bytes accessed | tf_op | source)
XLA Modules:
  0.0 256.8 jit_solution(11664577297712064873)
XLA Ops:
  6.5 4.3 %all-to-all-start = ((bf16[4,8,3584]{2,1,0:T(8,128)(2,1)}), bf16[4,8,3584]{2,1,0:T(8,128)(2,1)S(1)}, u32[]{:S(2)}, u32[]{:S(2)}) async-start(bf16[4,8,3584]{2,1,0:T(8,128)(2,1)} %bitcast.92), calls=%async_computation | async-start | bytes 458752 | tf_op jit(solution)/shard_map/all_to_all | solution.py:37
  13.3 1.4 scatter_custom_fusion
  15.9 1.4 all-to-all-done
  18.7 2.5 copy.28
  21.2 2.6 %reshape.243 = bf16[4,2,7168]{2,1,0:T(2,128)(2,1)} reshape(bf16[3584,2,8]{2,1,0:T(2,128)(2,1)S(1)} %bitcast.81) | data formatting | bytes 229376
  23.8 3.4 %all-to-all-start.1 = ((bf16[4,2,7168]{2,1,0:T(2,128)(2,1)}), bf16[4,2,7168]{2,1,0:T(2,128)(2,1)S(1)}, u32[]{:S(2)}, u32[]{:S(2)}) async-start(bf16[4,2,7168]{2,1,0:T(2,128)(2,1)} %reshape.243), calls=%async_computation.1 | async-start | bytes 229376 | tf_op jit(solution)/shard_map/all_to_all | solution.py:53
  27.2 5.9 %all-to-all-done.1 = bf16[4,2,7168]{2,1,0:T(2,128)(2,1)S(1)} async-done(((bf16[4,2,7168]{2,1,0:T(2,128)(2,1)}), bf16[4,2,7168]{2,1,0:T(2,128)(2,1)S(1)}, u32[]{:S(2)}, u32[]{:S(2)}) %all-to-all-start.1) | async-done | bytes 114720 | tf_op jit(solution)/shard_map/all_to_all | solution.py:53
  33.1 2.1 reshape.244
  36.3 2.1 gather_fusion
  38.6 1.5 broadcast_select_fusion
  40.1 17.4 %all-to-all-start.2 = ((bf16[128,4,896]{2,1,0:T(4,128)(2,1)}), bf16[128,4,896]{2,1,0:T(4,128)(2,1)S(1)}, u32[]{:S(2)}, u32[]{:S(2)}) async-start(bf16[128,4,896]{2,1,0:T(4,128)(2,1)} %broadcast_select_fusion), calls=%async_computation.2 | async-start | bytes 1835008 | tf_op jit(solution)/shard_map/all_to_all | solution.py:72
  57.6 2.8 %copy.35 = bf16[1,3584,256]{1,2,0:T(8,128)(2,1)S(1)} copy(bf16[1,3584,256]{2,1,0:T(8,128)(2,1)} %param.10) | data formatting | bytes 3670016 | tf_op args[3]
  60.3 1.9 fusion.13
  62.2 2.5 collective-permute-start
  64.7 4.0 %collective-permute-start.1 = (bf16[2,896,256]{1,2,0:T(8,128)(2,1)S(1)}, bf16[2,896,256]{1,2,0:T(8,128)(2,1)S(1)}, u32[]{:S(2)}, u32[]{:S(2)}) collective-permute-start(bf16[2,896,256]{1,2,0:T(8,128)(2,1)S(1)} %get-tuple-element.13), channel_id=1, source_target_pairs={{0,2},{1,3},{2,0},{3,1},{4,6},{5,7},{6,4},{7,5},{8,10},{9,11},{10,... | collective-permute-start | bytes 2752520 | tf_op jit(solution)/shard_map/ppermute | solution.py:33
  68.7 3.0 %collective-permute-start.2 = (bf16[2,896,256]{1,2,0:T(8,128)(2,1)S(1)}, bf16[2,896,256]{1,2,0:T(8,128)(2,1)S(1)}, u32[]{:S(2)}, u32[]{:S(2)}) collective-permute-start(bf16[2,896,256]{1,2,0:T(8,128)(2,1)S(1)} %get-tuple-element.14), channel_id=1, source_target_pairs={{0,3},{1,0},{2,1},{3,2},{4,7},{5,4},{6,5},{7,6},{8,11},{9,8},{10,9... | collective-permute-start | bytes 2752520 | tf_op jit(solution)/shard_map/ppermute | solution.py:33
  71.7 35.7 %collective-permute-done = bf16[2,896,256]{1,2,0:T(8,128)(2,1)S(1)} collective-permute-done((bf16[2,896,256]{1,2,0:T(8,128)(2,1)S(1)}, bf16[2,896,256]{1,2,0:T(8,128)(2,1)S(1)}, u32[]{:S(2)}, u32[]{:S(2)}) %collective-permute-start) | collective-permute-done | bytes 917536 | tf_op jit(solution)/shard_map/ppermute | solution.py:33
  107.4 2.5 collective-permute-done.2
  109.9 2.1 pad_maximum_fusion
  112.0 4.8 %gather_fusion.1 = bf16[4,2,896,256]{2,3,1,0:T(8,128)(2,1)} fusion(bf16[4,2,896,256]{2,3,1,0:T(8,128)(2,1)} %pad_maximum_fusion, s32[1024]{0:T(1024)S(1)} %pad_clamp_fusion.1), kind=kCustom, calls=%fused_computation.1 | custom fusion | bytes 7340048 | tf_op jit(solution)/shard_map/gather | solution.py:35
  116.8 2.4 slice_bitcast_fusion.11
  119.4 3.3 %fusion.8 = bf16[512,1024]{1,0:T(8,128)(2,1)} fusion(bf16[512,896]{1,0:T(8,128)(2,1)S(1)} %reshape.203, bf16[896,256]{0,1:T(8,128)(2,1)S(1)} %get-tuple-element.8, bf16[896,256]{0,1:T(8,128)(2,1)S(1)} %get-tuple-element.9, bf16[896,256]{0,1:T(8,128)(2,1)} %get-tuple-element.10, bf16[896,256]{0,1:T(8,128)(2,1)S(1)} %get-tuple-element.7), kind=kOutput, calls=%fused_computation.22 | convolution fusion | flops 947388416 | bytes 3801088 | tf_op jit(solution)/shard_map/dot_general | solution.py:76
  122.7 29.7 %reduce-scatter.2.cloned.1.call-done = bf16[512,256]{1,0:T(8,128)(2,1)} async-done(((bf16[512,1024]{1,0:T(8,128)(2,1)}), bf16[512,256]{1,0:T(8,128)(2,1)}) %reduce-scatter.2.cloned.1.call-update) | async-done | bytes 262160 | tf_op jit(solution)/shard_map/reduce_scatter | solution.py:77
  152.4 1.8 fusion.20
  154.3 30.8 %all-gather.2.cloned.1.call-done = bf16[512,1024]{1,0:T(8,128)(2,1)} async-done(((bf16[512,256]{1,0:T(8,128)(2,1)}), bf16[512,1024]{1,0:T(8,128)(2,1)}) %all-gather.2.cloned.1.call-update) | async-done | bytes 1048592 | tf_op jit(solution)/shard_map/all_gather | solution.py:81
  185.1 1.5 convolution_convert_fusion.2
  186.6 1.5 convolution_convert_fusion.1
  188.2 1.5 convolution_convert_fusion
  189.7 1.7 add_convert_fusion
  192.6 14.2 %all-to-all-start.3 = ((bf16[128,4,896]{2,1,0:T(4,128)(2,1)}), bf16[128,4,896]{2,1,0:T(4,128)(2,1)S(1)}, u32[]{:S(2)}, u32[]{:S(2)}) async-start(bf16[128,4,896]{2,1,0:T(4,128)(2,1)} %reshape.204), calls=%async_computation.4 | async-start | bytes 1835008 | tf_op jit(solution)/shard_map/all_to_all | solution.py:93
  206.8 28.5 %all-to-all-done.3 = bf16[128,4,896]{2,1,0:T(4,128)(2,1)S(1)} async-done(((bf16[128,4,896]{2,1,0:T(4,128)(2,1)}), bf16[128,4,896]{2,1,0:T(4,128)(2,1)S(1)}, u32[]{:S(2)}, u32[]{:S(2)}) %all-to-all-start.3) | async-done | bytes 917536 | tf_op jit(solution)/shard_map/all_to_all | solution.py:93
  237.1 12.2 %all_gather.7 = bf16[32,3584]{1,0:T(8,128)(2,1)S(1)} all-gather(bf16[32,896]{1,0:T(8,128)(2,1)S(1)} %fusion.33), channel_id=1, replica_groups=mesh['expert'=128,'tensor'=4] {'tensor'}, dimensions={1}, use_global_device_ids=true | all-gather | bytes 286720 | tf_op jit(solution)/shard_map/all_gather | solution.py:98
  (55 shorter events, 10.3 us)
Async XLA Ops:
  6.5 10.8 %all-to-all-start = ((bf16[4,8,3584]{2,1,0:T(8,128)(2,1)}), bf16[4,8,3584]{2,1,0:T(8,128)(2,1)S(1)}, u32[]{:S(2)}, u32[]{:S(2)}) async-start(bf16[4,8,3584]{2,1,0:T(8,128)(2,1)} %bitcast.92), calls=%async_computation | async-start | bytes 458752 | tf_op jit(solution)/shard_map/all_to_all | solution.py:37
  23.8 9.3 %all-to-all-start.1 = ((bf16[4,2,7168]{2,1,0:T(2,128)(2,1)}), bf16[4,2,7168]{2,1,0:T(2,128)(2,1)S(1)}, u32[]{:S(2)}, u32[]{:S(2)}) async-start(bf16[4,2,7168]{2,1,0:T(2,128)(2,1)} %reshape.243), calls=%async_computation.1 | async-start | bytes 229376 | tf_op jit(solution)/shard_map/all_to_all | solution.py:53
  40.1 79.1 %all-to-all-start.2 = ((bf16[128,4,896]{2,1,0:T(4,128)(2,1)}), bf16[128,4,896]{2,1,0:T(4,128)(2,1)S(1)}, u32[]{:S(2)}, u32[]{:S(2)}) async-start(bf16[128,4,896]{2,1,0:T(4,128)(2,1)} %broadcast_select_fusion), calls=%async_computation.2 | async-start | bytes 1835008 | tf_op jit(solution)/shard_map/all_to_all | solution.py:72
  57.5 95.0 %reduce-scatter.2.cloned.1.call-start = ((), (), s32[]{:S(2)}) async-start(), calls=%async_computation.5 | async-start | bytes 1310720 | tf_op jit(solution)/shard_map/reduce_scatter | solution.py:77
  62.2 45.1 %collective-permute-start = (bf16[2,896,256]{1,2,0:T(8,128)(2,1)S(1)}, bf16[2,896,256]{1,2,0:T(8,128)(2,1)S(1)}, u32[]{:S(2)}, u32[]{:S(2)}) collective-permute-start(bf16[2,896,256]{1,2,0:T(8,128)(2,1)S(1)} %get-tuple-element.12), channel_id=1, source_target_pairs={{0,1},{1,2},{2,3},{3,0},{4,5},{5,6},{6,7},{7,4},{8,9},{9,10},{10,1... | collective-permute-start | bytes 2752520 | tf_op jit(solution)/shard_map/ppermute | solution.py:33
  64.7 42.7 %collective-permute-start.1 = (bf16[2,896,256]{1,2,0:T(8,128)(2,1)S(1)}, bf16[2,896,256]{1,2,0:T(8,128)(2,1)S(1)}, u32[]{:S(2)}, u32[]{:S(2)}) collective-permute-start(bf16[2,896,256]{1,2,0:T(8,128)(2,1)S(1)} %get-tuple-element.13), channel_id=1, source_target_pairs={{0,2},{1,3},{2,0},{3,1},{4,6},{5,7},{6,4},{7,5},{8,10},{9,11},{10,... | collective-permute-start | bytes 2752520 | tf_op jit(solution)/shard_map/ppermute | solution.py:33
  68.7 41.2 %collective-permute-start.2 = (bf16[2,896,256]{1,2,0:T(8,128)(2,1)S(1)}, bf16[2,896,256]{1,2,0:T(8,128)(2,1)S(1)}, u32[]{:S(2)}, u32[]{:S(2)}) collective-permute-start(bf16[2,896,256]{1,2,0:T(8,128)(2,1)S(1)} %get-tuple-element.14), channel_id=1, source_target_pairs={{0,3},{1,0},{2,1},{3,2},{4,7},{5,4},{6,5},{7,6},{8,11},{9,8},{10,9... | collective-permute-start | bytes 2752520 | tf_op jit(solution)/shard_map/ppermute | solution.py:33
  122.7 62.4 %all-gather.2.cloned.1.call-start = ((), (), s32[]{:S(2)}) async-start(), calls=%async_computation.6 | async-start | bytes 1310720 | tf_op jit(solution)/shard_map/all_gather | solution.py:81
  189.7 17.0 %copy-start = (f32[32,8]{0,1:T(8,128)S(1)}, f32[32,8]{0,1:T(8,128)}, u32[]{:S(2)}) copy-start(f32[32,8]{0,1:T(8,128)} %param.13) | copy-start | bytes 3076
  192.6 42.7 %all-to-all-start.3 = ((bf16[128,4,896]{2,1,0:T(4,128)(2,1)}), bf16[128,4,896]{2,1,0:T(4,128)(2,1)S(1)}, u32[]{:S(2)}, u32[]{:S(2)}) async-start(bf16[128,4,896]{2,1,0:T(4,128)(2,1)} %reshape.204), calls=%async_computation.4 | async-start | bytes 1835008 | tf_op jit(solution)/shard_map/all_to_all | solution.py:93
Sparse Core Ops, SparseCore 0:
  122.8 29.5 reduce-scatter.1
  154.5 30.4 all-gather.1

commit v3 on v2

--- a/solution.py
+++ b/solution.py
@@ -21,7 +21,6 @@
     slot_count = capacity(group_tokens, top_count, expert_count)
     block_count = model_width // QB
     w_stack = jnp.stack([w_in[0], w_out[0].T])
-    hidden_quarter = w_stack.shape[2]
     width_quarter = model_width // tensor_count
     own = lax.axis_index("tensor")
     pieces = [lax.dynamic_slice_in_dim(w_stack, own * width_quarter, width_quarter, axis=1)]
@@ -33,7 +32,7 @@
         pieces.append(lax.ppermute(chunk, "tensor", ring))
     by_shift = jnp.stack(pieces)
     w_blocks = by_shift[(own - jnp.arange(tensor_count)) % tensor_count]
-    w_in_d = jnp.concatenate([w_blocks[j, 0] for j in range(tensor_count)], axis=1)
+
     head_terms = lax.all_to_all(
         attn_partial[0].reshape(tensor_count, -1, model_width), "tensor", split_axis=0, concat_axis=0
     )
@@ -73,17 +72,18 @@
     sources = recv_rows.shape[0]
     quarter = recv_rows.shape[2]
     rows = recv_rows.reshape(sources * slot_count, quarter)
-    pre_partial = jnp.dot(rows, w_in_d, preferred_element_type=jnp.float32)
-    pre_value = lax.psum_scatter(
-        pre_partial.astype(jnp.bfloat16), "tensor", scatter_dimension=1, tiled=True
-    ).astype(jnp.float32)
+    pre_blocks = jnp.einsum(
+        "rd,jdh->jrh", rows, w_blocks[:, 0], preferred_element_type=jnp.float32
+    ).astype(jnp.bfloat16)
+    pre_terms = lax.all_to_all(pre_blocks, "tensor", split_axis=0, concat_axis=0)
+    pre_value = jnp.sum(pre_terms.astype(jnp.float32), axis=0)
     hidden_part = jax.nn.silu(pre_value).astype(jnp.bfloat16)
-    hidden = lax.all_gather(hidden_part, "tensor", axis=1, tiled=True)
+    hidden_copies = jnp.broadcast_to(hidden_part[None], (tensor_count,) + hidden_part.shape)
+    hidden_blocks = lax.all_to_all(hidden_copies, "tensor", split_axis=0, concat_axis=0)
     summed = jnp.zeros((rows.shape[0], quarter), jnp.float32)
     for lane in range(tensor_count):
-        lo = lane * hidden_quarter
         term = lax.dot_general(
-            hidden[:, lo : lo + hidden_quarter],
+            hidden_blocks[lane],
             w_blocks[lane, 1],
             (((1,), (1,)), ((), ())),
             preferred_element_type=jnp.float32,
@@ -95,7 +95,9 @@
     picked = flat_back[target].astype(jnp.float32) * gate_weights.reshape(-1)[:, None]
     mixture = jnp.sum(picked.reshape(group_tokens, top_count, quarter), axis=1)
     out_part = (group_resid.astype(jnp.float32) + mixture).astype(jnp.bfloat16)
-    return lax.all_gather(out_part, "tensor", axis=1, tiled=True)
+    out_copies = jnp.broadcast_to(out_part[None], (tensor_count,) + out_part.shape)
+    out_blocks = lax.all_to_all(out_copies, "tensor", split_axis=0, concat_axis=0)
+    return out_blocks.transpose(1, 0, 2).reshape(group_tokens, model_width)
 
 
 def solution(mesh):

time: 258 us -> 212 us (0.82)
  the two profiles are of different devices: /device:TPU:8 before, /device:TPU:1 now
where the time goes in v3:
time: 212 us; the launch traced here: 211 us
  waiting for transfers between devices  71.4 us (34%)
  starting transfers between devices  53.2 us (25%)
  blocking collectives  43.4 us (20%)
  local copies, waits for them, and re-layouts  25 us (12%)
  matrix products  8.92 us (4%)
  other arithmetic  8.23 us (4%)
    ppermute x3, waiting for transfers between devices, layer(): pieces.append(lax.ppermute(chunk, 'tensor', ring))  37.9 us
    all_to_all x1, waiting for transfers between devices, layer(): lax.all_to_all(expert_out, 'expert', split_axis=0, concat_axis=0, tiled=T...  28.5 us
    all_to_all x1, starting transfers between devices, layer(): lax.all_to_all(row_block, 'expert', split_axis=0, concat_axis=0, tiled=True)  19.6 us
    all_to_all x1, blocking collectives, layer(): lax.all_to_all(pre_blocks, 'tensor', split_axis=0, concat_axis=0)  18.6 us
    all_to_all x1, starting transfers between devices, layer(): lax.all_to_all(expert_out, 'expert', split_axis=0, concat_axis=0, tiled=T...  16.1 us
    all_to_all x1, blocking collectives, layer(): lax.all_to_all(hidden_copies, 'tensor', split_axis=0, concat_axis=0)  15.7 us
    all_to_all x1, blocking collectives, layer(): lax.all_to_all(out_copies, 'tensor', split_axis=0, concat_axis=0)  9.08 us
    ppermute x3, starting transfers between devices, layer(): pieces.append(lax.ppermute(chunk, 'tensor', ring))  8.6 us
  transfers between devices with their start and end apart: 7, of which 6 were waited for; matrix products, arithmetic and copies ran while one was open for 8% of the time, Pallas kernels for 0%

profile of v3, /device:TPU:1, one launch (start us, length us, event | category | flops | bytes accessed | tf_op | source)
XLA Modules:
  0.0 210.6 jit_solution(15195411164287229123)
XLA Ops:
  0.0 5.0 %all-to-all-start = ((bf16[4,8,3584]{2,1,0:T(8,128)(2,1)}), bf16[4,8,3584]{2,1,0:T(8,128)(2,1)S(1)}, u32[]{:S(2)}, u32[]{:S(2)}) async-start(bf16[4,8,3584]{2,1,0:T(8,128)(2,1)} %bitcast.110), calls=%async_computation | async-start | bytes 458752 | tf_op jit(solution)/shard_map/all_to_all | solution.py:36
  7.4 1.4 scatter_custom_fusion
  10.9 2.5 %copy.31 = bf16[2,8,3584]{1,0,2:T(2,128)(2,1)S(1)} copy(bf16[2,8,3584]{2,1,0:T(8,128)(2,1)S(1)} %pad_maximum_fusion.1) | data formatting | bytes 229376 | tf_op jit(solution)/shard_map/stack | solution.py:51
  13.4 2.6 %reshape.266 = bf16[4,2,7168]{2,1,0:T(2,128)(2,1)} reshape(bf16[3584,2,8]{2,1,0:T(2,128)(2,1)S(1)} %bitcast.99) | data formatting | bytes 229376
  16.0 4.0 %all-to-all-start.1 = ((bf16[4,2,7168]{2,1,0:T(2,128)(2,1)}), bf16[4,2,7168]{2,1,0:T(2,128)(2,1)S(1)}, u32[]{:S(2)}, u32[]{:S(2)}) async-start(bf16[4,2,7168]{2,1,0:T(2,128)(2,1)} %reshape.266), calls=%async_computation.1 | async-start | bytes 229376 | tf_op jit(solution)/shard_map/all_to_all | solution.py:52
  19.9 4.7 %all-to-all-done.1 = bf16[4,2,7168]{2,1,0:T(2,128)(2,1)S(1)} async-done(((bf16[4,2,7168]{2,1,0:T(2,128)(2,1)}), bf16[4,2,7168]{2,1,0:T(2,128)(2,1)S(1)}, u32[]{:S(2)}, u32[]{:S(2)}) %all-to-all-start.1) | async-done | bytes 114720 | tf_op jit(solution)/shard_map/all_to_all | solution.py:52
  24.7 2.1 %reshape.267 = bf16[3584,2,8]{2,1,0:T(2,128)(2,1)S(1)} reshape(bf16[4,2,7168]{2,1,0:T(2,128)(2,1)S(1)} %all-to-all-done.1) | data formatting | bytes 229376
  28.0 2.1 gather_fusion.1
  30.2 1.5 broadcast_select_fusion
  31.7 19.6 %all-to-all-start.2 = ((bf16[128,4,896]{2,1,0:T(4,128)(2,1)}), bf16[128,4,896]{2,1,0:T(4,128)(2,1)S(1)}, u32[]{:S(2)}, u32[]{:S(2)}) async-start(bf16[128,4,896]{2,1,0:T(4,128)(2,1)} %broadcast_select_fusion), calls=%async_computation.2 | async-start | bytes 1835008 | tf_op jit(solution)/shard_map/all_to_all | solution.py:71
  51.3 2.9 %copy.33 = bf16[1,256,3584]{1,2,0:T(8,128)(2,1)S(1)} copy(bf16[1,256,3584]{2,1,0:T(8,128)(2,1)} %param.11) | data formatting | bytes 3670016 | tf_op args[4]
  54.2 1.7 fusion.5
  55.9 2.2 %collective-permute-start = (bf16[2,896,256]{2,1,0:T(8,128)(2,1)S(1)}, bf16[2,896,256]{2,1,0:T(8,128)(2,1)S(1)}, u32[]{:S(2)}, u32[]{:S(2)}) collective-permute-start(bf16[2,896,256]{2,1,0:T(8,128)(2,1)S(1)} %get-tuple-element.8), channel_id=1, source_target_pairs={{0,1},{1,2},{2,3},{3,0},{4,5},{5,6},{6,7},{7,4},{8,9},{9,10},{10,1... | collective-permute-start | bytes 2752520 | tf_op jit(solution)/shard_map/ppermute | solution.py:32
  58.1 3.7 %collective-permute-start.1 = (bf16[2,896,256]{2,1,0:T(8,128)(2,1)S(1)}, bf16[2,896,256]{2,1,0:T(8,128)(2,1)S(1)}, u32[]{:S(2)}, u32[]{:S(2)}) collective-permute-start(bf16[2,896,256]{2,1,0:T(8,128)(2,1)S(1)} %get-tuple-element.9), channel_id=1, source_target_pairs={{0,2},{1,3},{2,0},{3,1},{4,6},{5,7},{6,4},{7,5},{8,10},{9,11},{10,... | collective-permute-start | bytes 2752520 | tf_op jit(solution)/shard_map/ppermute | solution.py:32
  61.8 2.7 %collective-permute-start.2 = (bf16[2,896,256]{2,1,0:T(8,128)(2,1)S(1)}, bf16[2,896,256]{2,1,0:T(8,128)(2,1)S(1)}, u32[]{:S(2)}, u32[]{:S(2)}) collective-permute-start(bf16[2,896,256]{2,1,0:T(8,128)(2,1)S(1)} %get-tuple-element.10), channel_id=1, source_target_pairs={{0,3},{1,0},{2,1},{3,2},{4,7},{5,4},{6,5},{7,6},{8,11},{9,8},{10,9... | collective-permute-start | bytes 2752520 | tf_op jit(solution)/shard_map/ppermute | solution.py:32
  64.6 16.1 %collective-permute-done = bf16[2,896,256]{2,1,0:T(8,128)(2,1)S(1)} collective-permute-done((bf16[2,896,256]{2,1,0:T(8,128)(2,1)S(1)}, bf16[2,896,256]{2,1,0:T(8,128)(2,1)S(1)}, u32[]{:S(2)}, u32[]{:S(2)}) %collective-permute-start) | collective-permute-done | bytes 917536 | tf_op jit(solution)/shard_map/ppermute | solution.py:32
  80.7 18.5 %collective-permute-done.1 = bf16[2,896,256]{2,1,0:T(8,128)(2,1)S(1)} collective-permute-done((bf16[2,896,256]{2,1,0:T(8,128)(2,1)S(1)}, bf16[2,896,256]{2,1,0:T(8,128)(2,1)S(1)}, u32[]{:S(2)}, u32[]{:S(2)}) %collective-permute-start.1) | collective-permute-done | bytes 917536 | tf_op jit(solution)/shard_map/ppermute | solution.py:32
  99.2 3.3 %collective-permute-done.2 = bf16[2,896,256]{2,1,0:T(8,128)(2,1)S(1)} collective-permute-done((bf16[2,896,256]{2,1,0:T(8,128)(2,1)S(1)}, bf16[2,896,256]{2,1,0:T(8,128)(2,1)S(1)}, u32[]{:S(2)}, u32[]{:S(2)}) %collective-permute-start.2) | collective-permute-done | bytes 917536 | tf_op jit(solution)/shard_map/ppermute | solution.py:32
  102.5 2.0 pad_maximum_fusion
  104.5 4.6 %gather_fusion = bf16[4,2,896,256]{3,2,1,0:T(8,128)(2,1)} fusion(bf16[4,2,896,256]{3,2,1,0:T(8,128)(2,1)} %pad_maximum_fusion, s32[1024]{0:T(1024)S(1)} %pad_clamp_fusion.2), kind=kCustom, calls=%fused_computation | custom fusion | bytes 7340048 | tf_op jit(solution)/shard_map/gather | solution.py:34
  109.3 2.8 %fusion.2 = bf16[4,512,256]{1,2,0:T(8,128)(2,1)S(1)} fusion(bf16[512,896,1]{1,0,2:T(8,128)(2,1)S(1)} %reshape.262, bf16[4,2,896,256]{3,2,1,0:T(8,128)(2,1)} %gather_fusion), kind=kOutput, calls=%fused_computation.22 | convolution fusion | flops 940048384 | bytes 3801088 | tf_op jit(solution)/shard_map/rd,jdh->jrh/dot_general | solution.py:75
  112.1 18.6 %all_to_all.45 = bf16[4,512,256]{1,2,0:T(8,128)(2,1)S(1)} all-to-all(bf16[4,512,256]{1,2,0:T(8,128)(2,1)S(1)} %fusion.2), channel_id=1, replica_groups=mesh['expert'=128,'tensor'=4] {'tensor'}, dimensions={0} | all-to-all | bytes 2097152 | tf_op jit(solution)/shard_map/all_to_all | solution.py:78
  131.3 15.7 %all_to_all.46 = bf16[4,512,256]{2,1,0:T(8,128)(2,1)S(1)} all-to-all(bf16[4,512,256]{2,1,0:T(8,128)(2,1)S(1)} %broadcast_in_dim.21), channel_id=1, replica_groups=mesh['expert'=128,'tensor'=4] {'tensor'}, dimensions={0} | all-to-all | bytes 2097152 | tf_op jit(solution)/shard_map/all_to_all | solution.py:82
  147.0 1.5 convolution_convert_fusion.2
  148.4 1.5 convolution_convert_fusion.1
  149.9 1.5 convolution_convert_fusion
  151.4 1.7 add_convert_fusion
  153.1 1.1 reshape.224
  154.2 16.1 %all-to-all-start.5 = ((bf16[128,4,896]{2,1,0:T(4,128)(2,1)}), bf16[128,4,896]{2,1,0:T(4,128)(2,1)S(1)}, u32[]{:S(2)}, u32[]{:S(2)}) async-start(bf16[128,4,896]{2,1,0:T(4,128)(2,1)} %reshape.224), calls=%async_computation.5 | async-start | bytes 1835008 | tf_op jit(solution)/shard_map/all_to_all | solution.py:93
  170.5 28.5 %all-to-all-done.5 = bf16[128,4,896]{2,1,0:T(4,128)(2,1)S(1)} async-done(((bf16[128,4,896]{2,1,0:T(4,128)(2,1)}), bf16[128,4,896]{2,1,0:T(4,128)(2,1)S(1)}, u32[]{:S(2)}, u32[]{:S(2)}) %all-to-all-start.5) | async-done | bytes 917536 | tf_op jit(solution)/shard_map/all_to_all | solution.py:93
  199.2 1.2 gather_fusion.2
  200.8 9.1 %all_to_all.47 = bf16[4,32,896]{2,1,0:T(8,128)(2,1)S(1)} all-to-all(bf16[4,32,896]{2,1,0:T(8,128)(2,1)S(1)} %broadcast_in_dim.22), channel_id=1, replica_groups=mesh['expert'=128,'tensor'=4] {'tensor'}, dimensions={0} | all-to-all | bytes 458752 | tf_op jit(solution)/shard_map/all_to_all | solution.py:99
  (56 shorter events, 7.8 us)
Async XLA Ops:
  0.0 10.4 %copy-start = (bf16[8,3584]{1,0:T(8,128)(2,1)S(1)}, bf16[8,3584]{1,0:T(8,128)(2,1)}, u32[]{:S(2)}) copy-start(bf16[8,3584]{1,0:T(8,128)(2,1)} %param.8) | copy-start | bytes 172036
  0.0 10.3 %all-to-all-start = ((bf16[4,8,3584]{2,1,0:T(8,128)(2,1)}), bf16[4,8,3584]{2,1,0:T(8,128)(2,1)S(1)}, u32[]{:S(2)}, u32[]{:S(2)}) async-start(bf16[4,8,3584]{2,1,0:T(8,128)(2,1)} %bitcast.110), calls=%async_computation | async-start | bytes 458752 | tf_op jit(solution)/shard_map/all_to_all | solution.py:36
  16.0 8.7 %all-to-all-start.1 = ((bf16[4,2,7168]{2,1,0:T(2,128)(2,1)}), bf16[4,2,7168]{2,1,0:T(2,128)(2,1)S(1)}, u32[]{:S(2)}, u32[]{:S(2)}) async-start(bf16[4,2,7168]{2,1,0:T(2,128)(2,1)} %reshape.266), calls=%async_computation.1 | async-start | bytes 229376 | tf_op jit(solution)/shard_map/all_to_all | solution.py:52
  31.7 77.4 %all-to-all-start.2 = ((bf16[128,4,896]{2,1,0:T(4,128)(2,1)}), bf16[128,4,896]{2,1,0:T(4,128)(2,1)S(1)}, u32[]{:S(2)}, u32[]{:S(2)}) async-start(bf16[128,4,896]{2,1,0:T(4,128)(2,1)} %broadcast_select_fusion), calls=%async_computation.2 | async-start | bytes 1835008 | tf_op jit(solution)/shard_map/all_to_all | solution.py:71
  55.9 24.7 %collective-permute-start = (bf16[2,896,256]{2,1,0:T(8,128)(2,1)S(1)}, bf16[2,896,256]{2,1,0:T(8,128)(2,1)S(1)}, u32[]{:S(2)}, u32[]{:S(2)}) collective-permute-start(bf16[2,896,256]{2,1,0:T(8,128)(2,1)S(1)} %get-tuple-element.8), channel_id=1, source_target_pairs={{0,1},{1,2},{2,3},{3,0},{4,5},{5,6},{6,7},{7,4},{8,9},{9,10},{10,1... | collective-permute-start | bytes 2752520 | tf_op jit(solution)/shard_map/ppermute | solution.py:32
  58.1 41.0 %collective-permute-start.1 = (bf16[2,896,256]{2,1,0:T(8,128)(2,1)S(1)}, bf16[2,896,256]{2,1,0:T(8,128)(2,1)S(1)}, u32[]{:S(2)}, u32[]{:S(2)}) collective-permute-start(bf16[2,896,256]{2,1,0:T(8,128)(2,1)S(1)} %get-tuple-element.9), channel_id=1, source_target_pairs={{0,2},{1,3},{2,0},{3,1},{4,6},{5,7},{6,4},{7,5},{8,10},{9,11},{10,... | collective-permute-start | bytes 2752520 | tf_op jit(solution)/shard_map/ppermute | solution.py:32
  61.8 40.6 %collective-permute-start.2 = (bf16[2,896,256]{2,1,0:T(8,128)(2,1)S(1)}, bf16[2,896,256]{2,1,0:T(8,128)(2,1)S(1)}, u32[]{:S(2)}, u32[]{:S(2)}) collective-permute-start(bf16[2,896,256]{2,1,0:T(8,128)(2,1)S(1)} %get-tuple-element.10), channel_id=1, source_target_pairs={{0,3},{1,0},{2,1},{3,2},{4,7},{5,4},{6,5},{7,6},{8,11},{9,8},{10,9... | collective-permute-start | bytes 2752520 | tf_op jit(solution)/shard_map/ppermute | solution.py:32
  153.1 17.3 %copy-start.1 = (f32[32,8]{0,1:T(8,128)S(1)}, f32[32,8]{0,1:T(8,128)}, u32[]{:S(2)}) copy-start(f32[32,8]{0,1:T(8,128)} %param.13) | copy-start | bytes 3076
  154.2 44.7 %all-to-all-start.5 = ((bf16[128,4,896]{2,1,0:T(4,128)(2,1)}), bf16[128,4,896]{2,1,0:T(4,128)(2,1)S(1)}, u32[]{:S(2)}, u32[]{:S(2)}) async-start(bf16[128,4,896]{2,1,0:T(4,128)(2,1)} %reshape.224), calls=%async_computation.5 | async-start | bytes 1835008 | tf_op jit(solution)/shard_map/all_to_all | solution.py:93

commit v4 on v3

--- a/solution.py
+++ b/solution.py
@@ -48,9 +48,12 @@
     expert_input = (
         (quantized.astype(jnp.float32) * scale_wide).reshape(-1, model_width).astype(jnp.bfloat16)
     )
-    both_rows = jnp.stack([expert_input, residual])
-    both = lax.all_to_all(both_rows, "tensor", split_axis=2, concat_axis=1, tiled=True)
-    group_input, group_resid = both[0], both[1]
+    token_rows = expert_input.shape[0]
+    both_rows = jnp.concatenate([expert_input, residual], axis=0)
+    both_rows = both_rows.reshape(2 * token_rows, tensor_count, -1).transpose(1, 0, 2)
+    both = lax.all_to_all(both_rows, "tensor", split_axis=0, concat_axis=0)
+    group_input = both[:, :token_rows].reshape(group_tokens, -1)
+    group_resid = both[:, token_rows:].reshape(group_tokens, -1)
     pair_expert = routes.reshape(-1)
     onehot = (pair_expert[:, None] == jnp.arange(expert_count, dtype=jnp.int32)[None, :]).astype(
         jnp.int32

time: 212 us -> 201 us (0.948)
  local copies, waits for them, and re-layouts: 25 us -> 17.3 us
    unnamed x10 -> x8, local copies, waits for them, and re-layouts: 8.5 us -> 3.74 us
    another operation x4 -> x3, local copies, waits for them, and re-layouts: 2.5 us -> 0.02 us  [the longest x1 2.48 us: layer(): both_rows = jnp.stack([expert_input, residual])]
where the time goes in v4:
time: 201 us; the launch traced here: 200 us
  waiting for transfers between devices  70.4 us (35%)
  starting transfers between devices  52.9 us (26%)
  blocking collectives  42.2 us (21%)
  local copies, waits for them, and re-layouts  17.3 us (9%)
  matrix products  8.92 us (4%)
  other arithmetic  8.23 us (4%)
    ppermute x3, waiting for transfers between devices, layer(): pieces.append(lax.ppermute(chunk, 'tensor', ring))  36.9 us
    all_to_all x1, waiting for transfers between devices, layer(): lax.all_to_all(expert_out, 'expert', split_axis=0, concat_axis=0, tiled=T...  28.5 us
    all_to_all x1, starting transfers between devices, layer(): lax.all_to_all(row_block, 'expert', split_axis=0, concat_axis=0, tiled=True)  19.6 us
    all_to_all x1, blocking collectives, layer(): lax.all_to_all(pre_blocks, 'tensor', split_axis=0, concat_axis=0)  17.1 us
    all_to_all x1, starting transfers between devices, layer(): lax.all_to_all(expert_out, 'expert', split_axis=0, concat_axis=0, tiled=T...  16 us
    all_to_all x1, blocking collectives, layer(): lax.all_to_all(hidden_copies, 'tensor', split_axis=0, concat_axis=0)  16 us
    all_to_all x1, blocking collectives, layer(): lax.all_to_all(out_copies, 'tensor', split_axis=0, concat_axis=0)  9.08 us
    ppermute x3, starting transfers between devices, layer(): pieces.append(lax.ppermute(chunk, 'tensor', ring))  8.41 us
  transfers between devices with their start and end apart: 7, of which 6 were waited for; matrix products, arithmetic and copies ran while one was open for 8% of the time, Pallas kernels for 0%

profile of v4, /device:TPU:1, one launch (start us, length us, event | category | flops | bytes accessed | tf_op | source)
XLA Modules:
  0.0 200.3 jit_solution(2251101085545567950)
XLA Ops:
  0.0 5.0 %all-to-all-start = ((bf16[4,8,3584]{2,1,0:T(8,128)(2,1)}), bf16[4,8,3584]{2,1,0:T(8,128)(2,1)S(1)}, u32[]{:S(2)}, u32[]{:S(2)}) async-start(bf16[4,8,3584]{2,1,0:T(8,128)(2,1)} %bitcast.104), calls=%async_computation | async-start | bytes 458752 | tf_op jit(solution)/shard_map/all_to_all | solution.py:36
  5.0 0.8 copy.34
  7.4 1.4 scatter_custom_fusion
  8.8 0.7 convert_element_type.118
  11.5 4.0 %all-to-all-start.1 = ((bf16[4,16,896]{2,1,0:T(8,128)(2,1)}), bf16[4,16,896]{2,1,0:T(8,128)(2,1)S(1)}, u32[]{:S(2)}, u32[]{:S(2)}) async-start(bf16[4,16,896]{2,1,0:T(8,128)(2,1)} %bitcast.92), calls=%async_computation.1 | async-start | bytes 229376 | tf_op jit(solution)/shard_map/all_to_all | solution.py:54
  15.5 4.7 %all-to-all-done.1 = bf16[4,16,896]{2,1,0:T(8,128)(2,1)S(1)} async-done(((bf16[4,16,896]{2,1,0:T(8,128)(2,1)}), bf16[4,16,896]{2,1,0:T(8,128)(2,1)S(1)}, u32[]{:S(2)}, u32[]{:S(2)}) %all-to-all-start.1) | async-done | bytes 114720 | tf_op jit(solution)/shard_map/all_to_all | solution.py:54
  20.2 2.0 %gather_fusion.1 = bf16[512,896]{1,0:T(8,128)(2,1)S(1)} fusion(bf16[32,896]{1,0:T(8,128)(2,1)S(1)} %slice_bitcast_fusion.22, s32[1024]{0:T(1024)S(1)} %pad_clamp_fusion.1), kind=kCustom, calls=%fused_computation.1 | custom fusion | bytes 1837056 | tf_op jit(solution)/shard_map/gather | solution.py:73
  22.5 1.5 broadcast_select_fusion
  24.0 19.6 %all-to-all-start.2 = ((bf16[128,4,896]{2,1,0:T(4,128)(2,1)}), bf16[128,4,896]{2,1,0:T(4,128)(2,1)S(1)}, u32[]{:S(2)}, u32[]{:S(2)}) async-start(bf16[128,4,896]{2,1,0:T(4,128)(2,1)} %broadcast_select_fusion), calls=%async_computation.2 | async-start | bytes 1835008 | tf_op jit(solution)/shard_map/all_to_all | solution.py:74
  43.6 2.9 %copy.31 = bf16[1,256,3584]{1,2,0:T(8,128)(2,1)S(1)} copy(bf16[1,256,3584]{2,1,0:T(8,128)(2,1)} %param.11) | data formatting | bytes 3670016 | tf_op args[4]
  46.5 1.7 fusion.5
  48.2 2.5 %collective-permute-start.1 = (bf16[2,896,256]{2,1,0:T(8,128)(2,1)S(1)}, bf16[2,896,256]{2,1,0:T(8,128)(2,1)S(1)}, u32[]{:S(2)}, u32[]{:S(2)}) collective-permute-start(bf16[2,896,256]{2,1,0:T(8,128)(2,1)S(1)} %get-tuple-element.9), channel_id=1, source_target_pairs={{0,2},{1,3},{2,0},{3,1},{4,6},{5,7},{6,4},{7,5},{8,10},{9,11},{10,... | collective-permute-start | bytes 2752520 | tf_op jit(solution)/shard_map/ppermute | solution.py:32
  50.7 4.0 %collective-permute-start.2 = (bf16[2,896,256]{2,1,0:T(8,128)(2,1)S(1)}, bf16[2,896,256]{2,1,0:T(8,128)(2,1)S(1)}, u32[]{:S(2)}, u32[]{:S(2)}) collective-permute-start(bf16[2,896,256]{2,1,0:T(8,128)(2,1)S(1)} %get-tuple-element.10), channel_id=1, source_target_pairs={{0,3},{1,0},{2,1},{3,2},{4,7},{5,4},{6,5},{7,6},{8,11},{9,8},{10,9... | collective-permute-start | bytes 2752520 | tf_op jit(solution)/shard_map/ppermute | solution.py:32
  54.7 1.9 collective-permute-start
  56.7 16.0 %collective-permute-done.1 = bf16[2,896,256]{2,1,0:T(8,128)(2,1)S(1)} collective-permute-done((bf16[2,896,256]{2,1,0:T(8,128)(2,1)S(1)}, bf16[2,896,256]{2,1,0:T(8,128)(2,1)S(1)}, u32[]{:S(2)}, u32[]{:S(2)}) %collective-permute-start.1) | collective-permute-done | bytes 917536 | tf_op jit(solution)/shard_map/ppermute | solution.py:32
  72.6 18.4 %collective-permute-done.2 = bf16[2,896,256]{2,1,0:T(8,128)(2,1)S(1)} collective-permute-done((bf16[2,896,256]{2,1,0:T(8,128)(2,1)S(1)}, bf16[2,896,256]{2,1,0:T(8,128)(2,1)S(1)}, u32[]{:S(2)}, u32[]{:S(2)}) %collective-permute-start.2) | collective-permute-done | bytes 917536 | tf_op jit(solution)/shard_map/ppermute | solution.py:32
  91.0 2.5 %collective-permute-done = bf16[2,896,256]{2,1,0:T(8,128)(2,1)S(1)} collective-permute-done((bf16[2,896,256]{2,1,0:T(8,128)(2,1)S(1)}, bf16[2,896,256]{2,1,0:T(8,128)(2,1)S(1)}, u32[]{:S(2)}, u32[]{:S(2)}) %collective-permute-start) | collective-permute-done | bytes 917536 | tf_op jit(solution)/shard_map/ppermute | solution.py:32
  93.5 2.0 %pad_maximum_fusion = bf16[4,2,896,256]{3,2,1,0:T(8,128)(2,1)} fusion(bf16[1,2,896,256]{3,2,1,0:T(8,128)(2,1)S(1)} %bitcast.98, bf16[1,2,896,256]{3,2,1,0:T(8,128)(2,1)S(1)} %bitcast.97, bf16[1,2,896,256]{3,2,1,0:T(8,128)(2,1)S(1)} %bitcast.99, bf16[1,2,896,256]{3,2,1,0:T(8,128)(2,1)S(1)} %get-tuple-element.7), kind=kLoop, calls=%fused_computation.12 | loop fusion | flops 5505024 | bytes 7340032 | tf_op jit(solution)/shard_map/stack | solution.py:33
  95.6 4.6 %gather_fusion = bf16[4,2,896,256]{3,2,1,0:T(8,128)(2,1)} fusion(bf16[4,2,896,256]{3,2,1,0:T(8,128)(2,1)} %pad_maximum_fusion, s32[1024]{0:T(1024)S(1)} %pad_clamp_fusion.2), kind=kCustom, calls=%fused_computation | custom fusion | bytes 7340048 | tf_op jit(solution)/shard_map/gather | solution.py:34
  100.4 2.8 %fusion.2 = bf16[4,512,256]{1,2,0:T(8,128)(2,1)S(1)} fusion(bf16[512,896,1]{1,0,2:T(8,128)(2,1)S(1)} %reshape.267, bf16[4,2,896,256]{3,2,1,0:T(8,128)(2,1)} %gather_fusion), kind=kOutput, calls=%fused_computation.22 | convolution fusion | flops 940048384 | bytes 3801088 | tf_op jit(solution)/shard_map/rd,jdh->jrh/dot_general | solution.py:78
  103.2 17.1 %all_to_all.35 = bf16[4,512,256]{1,2,0:T(8,128)(2,1)S(1)} all-to-all(bf16[4,512,256]{1,2,0:T(8,128)(2,1)S(1)} %fusion.2), channel_id=1, replica_groups=mesh['expert'=128,'tensor'=4] {'tensor'}, dimensions={0} | all-to-all | bytes 2097152 | tf_op jit(solution)/shard_map/all_to_all | solution.py:81
  120.8 16.0 %all_to_all.36 = bf16[4,512,256]{2,1,0:T(8,128)(2,1)S(1)} all-to-all(bf16[4,512,256]{2,1,0:T(8,128)(2,1)S(1)} %broadcast_in_dim.21), channel_id=1, replica_groups=mesh['expert'=128,'tensor'=4] {'tensor'}, dimensions={0} | all-to-all | bytes 2097152 | tf_op jit(solution)/shard_map/all_to_all | solution.py:85
  136.8 1.5 convolution_convert_fusion.2
  138.3 1.5 convolution_convert_fusion.1
  139.8 1.5 convolution_convert_fusion
  141.3 1.7 add_convert_fusion
  143.0 1.1 reshape.229
  144.1 16.0 %all-to-all-start.5 = ((bf16[128,4,896]{2,1,0:T(4,128)(2,1)}), bf16[128,4,896]{2,1,0:T(4,128)(2,1)S(1)}, u32[]{:S(2)}, u32[]{:S(2)}) async-start(bf16[128,4,896]{2,1,0:T(4,128)(2,1)} %reshape.229), calls=%async_computation.5 | async-start | bytes 1835008 | tf_op jit(solution)/shard_map/all_to_all | solution.py:96
  160.2 28.5 %all-to-all-done.5 = bf16[128,4,896]{2,1,0:T(4,128)(2,1)S(1)} async-done(((bf16[128,4,896]{2,1,0:T(4,128)(2,1)}), bf16[128,4,896]{2,1,0:T(4,128)(2,1)S(1)}, u32[]{:S(2)}, u32[]{:S(2)}) %all-to-all-start.5) | async-done | bytes 917536 | tf_op jit(solution)/shard_map/all_to_all | solution.py:96
  188.9 1.2 gather_fusion.2
  190.5 9.1 %all_to_all.37 = bf16[4,32,896]{2,1,0:T(8,128)(2,1)S(1)} all-to-all(bf16[4,32,896]{2,1,0:T(8,128)(2,1)S(1)} %broadcast_in_dim.22), channel_id=1, replica_groups=mesh['expert'=128,'tensor'=4] {'tensor'}, dimensions={0} | all-to-all | bytes 458752 | tf_op jit(solution)/shard_map/all_to_all | solution.py:102
  199.6 0.7 copy.43
  (53 shorter events, 5.2 us)
Async XLA Ops:
  0.0 10.4 %copy-start = (bf16[8,3584]{1,0:T(8,128)(2,1)S(1)}, bf16[8,3584]{1,0:T(8,128)(2,1)}, u32[]{:S(2)}) copy-start(bf16[8,3584]{1,0:T(8,128)(2,1)} %param.8) | copy-start | bytes 172036
  0.0 10.3 %all-to-all-start = ((bf16[4,8,3584]{2,1,0:T(8,128)(2,1)}), bf16[4,8,3584]{2,1,0:T(8,128)(2,1)S(1)}, u32[]{:S(2)}, u32[]{:S(2)}) async-start(bf16[4,8,3584]{2,1,0:T(8,128)(2,1)} %bitcast.104), calls=%async_computation | async-start | bytes 458752 | tf_op jit(solution)/shard_map/all_to_all | solution.py:36
  11.5 8.7 %all-to-all-start.1 = ((bf16[4,16,896]{2,1,0:T(8,128)(2,1)}), bf16[4,16,896]{2,1,0:T(8,128)(2,1)S(1)}, u32[]{:S(2)}, u32[]{:S(2)}) async-start(bf16[4,16,896]{2,1,0:T(8,128)(2,1)} %bitcast.92), calls=%async_computation.1 | async-start | bytes 229376 | tf_op jit(solution)/shard_map/all_to_all | solution.py:54
  24.0 76.2 %all-to-all-start.2 = ((bf16[128,4,896]{2,1,0:T(4,128)(2,1)}), bf16[128,4,896]{2,1,0:T(4,128)(2,1)S(1)}, u32[]{:S(2)}, u32[]{:S(2)}) async-start(bf16[128,4,896]{2,1,0:T(4,128)(2,1)} %broadcast_select_fusion), calls=%async_computation.2 | async-start | bytes 1835008 | tf_op jit(solution)/shard_map/all_to_all | solution.py:74
  48.2 24.5 %collective-permute-start.1 = (bf16[2,896,256]{2,1,0:T(8,128)(2,1)S(1)}, bf16[2,896,256]{2,1,0:T(8,128)(2,1)S(1)}, u32[]{:S(2)}, u32[]{:S(2)}) collective-permute-start(bf16[2,896,256]{2,1,0:T(8,128)(2,1)S(1)} %get-tuple-element.9), channel_id=1, source_target_pairs={{0,2},{1,3},{2,0},{3,1},{4,6},{5,7},{6,4},{7,5},{8,10},{9,11},{10,... | collective-permute-start | bytes 2752520 | tf_op jit(solution)/shard_map/ppermute | solution.py:32
  50.7 40.3 %collective-permute-start.2 = (bf16[2,896,256]{2,1,0:T(8,128)(2,1)S(1)}, bf16[2,896,256]{2,1,0:T(8,128)(2,1)S(1)}, u32[]{:S(2)}, u32[]{:S(2)}) collective-permute-start(bf16[2,896,256]{2,1,0:T(8,128)(2,1)S(1)} %get-tuple-element.10), channel_id=1, source_target_pairs={{0,3},{1,0},{2,1},{3,2},{4,7},{5,4},{6,5},{7,6},{8,11},{9,8},{10,9... | collective-permute-start | bytes 2752520 | tf_op jit(solution)/shard_map/ppermute | solution.py:32
  54.7 38.8 %collective-permute-start = (bf16[2,896,256]{2,1,0:T(8,128)(2,1)S(1)}, bf16[2,896,256]{2,1,0:T(8,128)(2,1)S(1)}, u32[]{:S(2)}, u32[]{:S(2)}) collective-permute-start(bf16[2,896,256]{2,1,0:T(8,128)(2,1)S(1)} %get-tuple-element.8), channel_id=1, source_target_pairs={{0,1},{1,2},{2,3},{3,0},{4,5},{5,6},{6,7},{7,4},{8,9},{9,10},{10,1... | collective-permute-start | bytes 2752520 | tf_op jit(solution)/shard_map/ppermute | solution.py:32
  143.0 17.2 %copy-start.1 = (f32[32,8]{0,1:T(8,128)S(1)}, f32[32,8]{0,1:T(8,128)}, u32[]{:S(2)}) copy-start(f32[32,8]{0,1:T(8,128)} %param.13) | copy-start | bytes 3076
  144.1 44.6 %all-to-all-start.5 = ((bf16[128,4,896]{2,1,0:T(4,128)(2,1)}), bf16[128,4,896]{2,1,0:T(4,128)(2,1)S(1)}, u32[]{:S(2)}, u32[]{:S(2)}) async-start(bf16[128,4,896]{2,1,0:T(4,128)(2,1)} %reshape.229), calls=%async_computation.5 | async-start | bytes 1835008 | tf_op jit(solution)/shard_map/all_to_all | solution.py:96

commit v5 on v4

--- a/solution.py
+++ b/solution.py
@@ -83,15 +83,10 @@
     hidden_part = jax.nn.silu(pre_value).astype(jnp.bfloat16)
     hidden_copies = jnp.broadcast_to(hidden_part[None], (tensor_count,) + hidden_part.shape)
     hidden_blocks = lax.all_to_all(hidden_copies, "tensor", split_axis=0, concat_axis=0)
-    summed = jnp.zeros((rows.shape[0], quarter), jnp.float32)
-    for lane in range(tensor_count):
-        term = lax.dot_general(
-            hidden_blocks[lane],
-            w_blocks[lane, 1],
-            (((1,), (1,)), ((), ())),
-            preferred_element_type=jnp.float32,
-        ).astype(jnp.bfloat16)
-        summed = summed + term.astype(jnp.float32)
+    terms = jnp.einsum(
+        "jrh,jdh->jrd", hidden_blocks, w_blocks[:, 1], preferred_element_type=jnp.float32
+    ).astype(jnp.bfloat16)
+    summed = jnp.sum(terms.astype(jnp.float32), axis=0)
     expert_out = summed.astype(jnp.bfloat16).reshape(sources, slot_count, quarter)
     returned = lax.all_to_all(expert_out, "expert", split_axis=0, concat_axis=0, tiled=True)
     flat_back = returned.reshape(expert_count * slot_count, quarter)

time: 201 us -> 199 us (0.990)
  matrix products: 8.92 us -> 5.67 us
    dot_general x4 -> x1, matrix products: 6.12 us -> 2.87 us  [layer(): jnp.einsum('jrh,jdh->jrd', hidden_blocks, w_blocks[:, 1], preferred_eleme...]
where the time goes in v5:
time: 199 us; the launch traced here: 198 us
  waiting for transfers between devices  70.4 us (35%)
  starting transfers between devices  52.6 us (26%)
  blocking collectives  42.2 us (21%)
  local copies, waits for them, and re-layouts  17.3 us (9%)
  other arithmetic  9.05 us (5%)
  matrix products  5.67 us (3%)
    ppermute x3, waiting for transfers between devices, layer(): pieces.append(lax.ppermute(chunk, 'tensor', ring))  36.9 us
    all_to_all x1, waiting for transfers between devices, layer(): lax.all_to_all(expert_out, 'expert', split_axis=0, concat_axis=0, tiled=T...  28.5 us
    all_to_all x1, starting transfers between devices, layer(): lax.all_to_all(row_block, 'expert', split_axis=0, concat_axis=0, tiled=True)  19.6 us
    all_to_all x1, blocking collectives, layer(): lax.all_to_all(pre_blocks, 'tensor', split_axis=0, concat_axis=0)  17.1 us
    all_to_all x1, blocking collectives, layer(): lax.all_to_all(hidden_copies, 'tensor', split_axis=0, concat_axis=0)  16 us
    all_to_all x1, starting transfers between devices, layer(): lax.all_to_all(expert_out, 'expert', split_axis=0, concat_axis=0, tiled=T...  15.8 us
    all_to_all x1, blocking collectives, layer(): lax.all_to_all(out_copies, 'tensor', split_axis=0, concat_axis=0)  9.08 us
    ppermute x3, starting transfers between devices, layer(): pieces.append(lax.ppermute(chunk, 'tensor', ring))  8.41 us
  transfers between devices with their start and end apart: 7, of which 6 were waited for; matrix products, arithmetic and copies ran while one was open for 8% of the time, Pallas kernels for 0%

profile of v5, /device:TPU:1, one launch (start us, length us, event | category | flops | bytes accessed | tf_op | source)
XLA Modules:
  0.0 197.5 jit_solution(7906963207413043869)
XLA Ops:
  0.0 4.8 %all-to-all-start = ((bf16[4,8,3584]{2,1,0:T(8,128)(2,1)}), bf16[4,8,3584]{2,1,0:T(8,128)(2,1)S(1)}, u32[]{:S(2)}, u32[]{:S(2)}) async-start(bf16[4,8,3584]{2,1,0:T(8,128)(2,1)} %bitcast.86), calls=%async_computation | async-start | bytes 458752 | tf_op jit(solution)/shard_map/all_to_all | solution.py:36
  4.8 0.8 copy.37
  5.8 0.7 broadcast_multiply_fusion
  7.3 1.4 scatter_custom_fusion
  8.7 0.7 convert_element_type.96
  10.2 1.0 fusion.13
  11.5 0.7 copy.50
  12.2 4.0 %all-to-all-start.1 = ((bf16[4,16,896]{2,1,0:T(8,128)(2,1)}), bf16[4,16,896]{2,1,0:T(8,128)(2,1)S(1)}, u32[]{:S(2)}, u32[]{:S(2)}) async-start(bf16[4,16,896]{2,1,0:T(8,128)(2,1)} %bitcast.74), calls=%async_computation.1 | async-start | bytes 229376 | tf_op jit(solution)/shard_map/all_to_all | solution.py:54
  16.2 4.7 %all-to-all-done.1 = bf16[4,16,896]{2,1,0:T(8,128)(2,1)S(1)} async-done(((bf16[4,16,896]{2,1,0:T(8,128)(2,1)}), bf16[4,16,896]{2,1,0:T(8,128)(2,1)S(1)}, u32[]{:S(2)}, u32[]{:S(2)}) %all-to-all-start.1) | async-done | bytes 114720 | tf_op jit(solution)/shard_map/all_to_all | solution.py:54
  20.9 2.0 %gather_fusion.1 = bf16[512,896]{1,0:T(8,128)(2,1)S(1)} fusion(bf16[32,896]{1,0:T(8,128)(2,1)S(1)} %slice_bitcast_fusion.8, s32[1024]{0:T(1024)S(1)} %pad_clamp_fusion.1), kind=kCustom, calls=%fused_computation.1 | custom fusion | bytes 1837056 | tf_op jit(solution)/shard_map/gather | solution.py:73
  23.2 1.5 broadcast_select_fusion
  24.6 19.6 %all-to-all-start.2 = ((bf16[128,4,896]{2,1,0:T(4,128)(2,1)}), bf16[128,4,896]{2,1,0:T(4,128)(2,1)S(1)}, u32[]{:S(2)}, u32[]{:S(2)}) async-start(bf16[128,4,896]{2,1,0:T(4,128)(2,1)} %broadcast_select_fusion), calls=%async_computation.2 | async-start | bytes 1835008 | tf_op jit(solution)/shard_map/all_to_all | solution.py:74
  44.3 2.9 %copy.34 = bf16[1,256,3584]{1,2,0:T(8,128)(2,1)S(1)} copy(bf16[1,256,3584]{2,1,0:T(8,128)(2,1)} %param.11) | data formatting | bytes 3670016 | tf_op args[4]
  47.2 1.7 fusion.5
  48.9 2.5 %collective-permute-start.1 = (bf16[2,896,256]{2,1,0:T(8,128)(2,1)S(1)}, bf16[2,896,256]{2,1,0:T(8,128)(2,1)S(1)}, u32[]{:S(2)}, u32[]{:S(2)}) collective-permute-start(bf16[2,896,256]{2,1,0:T(8,128)(2,1)S(1)} %get-tuple-element.9), channel_id=1, source_target_pairs={{0,2},{1,3},{2,0},{3,1},{4,6},{5,7},{6,4},{7,5},{8,10},{9,11},{10,... | collective-permute-start | bytes 2752520 | tf_op jit(solution)/shard_map/ppermute | solution.py:32
  51.4 4.0 %collective-permute-start.2 = (bf16[2,896,256]{2,1,0:T(8,128)(2,1)S(1)}, bf16[2,896,256]{2,1,0:T(8,128)(2,1)S(1)}, u32[]{:S(2)}, u32[]{:S(2)}) collective-permute-start(bf16[2,896,256]{2,1,0:T(8,128)(2,1)S(1)} %get-tuple-element.10), channel_id=1, source_target_pairs={{0,3},{1,0},{2,1},{3,2},{4,7},{5,4},{6,5},{7,6},{8,11},{9,8},{10,9... | collective-permute-start | bytes 2752520 | tf_op jit(solution)/shard_map/ppermute | solution.py:32
  55.4 1.9 collective-permute-start
  57.3 16.0 %collective-permute-done.1 = bf16[2,896,256]{2,1,0:T(8,128)(2,1)S(1)} collective-permute-done((bf16[2,896,256]{2,1,0:T(8,128)(2,1)S(1)}, bf16[2,896,256]{2,1,0:T(8,128)(2,1)S(1)}, u32[]{:S(2)}, u32[]{:S(2)}) %collective-permute-start.1) | collective-permute-done | bytes 917536 | tf_op jit(solution)/shard_map/ppermute | solution.py:32
  73.3 18.4 %collective-permute-done.2 = bf16[2,896,256]{2,1,0:T(8,128)(2,1)S(1)} collective-permute-done((bf16[2,896,256]{2,1,0:T(8,128)(2,1)S(1)}, bf16[2,896,256]{2,1,0:T(8,128)(2,1)S(1)}, u32[]{:S(2)}, u32[]{:S(2)}) %collective-permute-start.2) | collective-permute-done | bytes 917536 | tf_op jit(solution)/shard_map/ppermute | solution.py:32
  91.7 2.5 %collective-permute-done = bf16[2,896,256]{2,1,0:T(8,128)(2,1)S(1)} collective-permute-done((bf16[2,896,256]{2,1,0:T(8,128)(2,1)S(1)}, bf16[2,896,256]{2,1,0:T(8,128)(2,1)S(1)}, u32[]{:S(2)}, u32[]{:S(2)}) %collective-permute-start) | collective-permute-done | bytes 917536 | tf_op jit(solution)/shard_map/ppermute | solution.py:32
  94.2 2.0 %pad_maximum_fusion = bf16[4,2,896,256]{3,2,1,0:T(8,128)(2,1)} fusion(bf16[1,2,896,256]{3,2,1,0:T(8,128)(2,1)S(1)} %bitcast.80, bf16[1,2,896,256]{3,2,1,0:T(8,128)(2,1)S(1)} %bitcast.79, bf16[1,2,896,256]{3,2,1,0:T(8,128)(2,1)S(1)} %bitcast.81, bf16[1,2,896,256]{3,2,1,0:T(8,128)(2,1)S(1)} %get-tuple-element.7), kind=kLoop, calls=%fused_computation.12 | loop fusion | flops 5505024 | bytes 7340032 | tf_op jit(solution)/shard_map/stack | solution.py:33
  96.2 4.6 %gather_fusion = bf16[4,2,896,256]{3,2,1,0:T(8,128)(2,1)} fusion(bf16[4,2,896,256]{3,2,1,0:T(8,128)(2,1)} %pad_maximum_fusion, s32[1024]{0:T(1024)S(1)} %pad_clamp_fusion.2), kind=kCustom, calls=%fused_computation | custom fusion | bytes 7340048 | tf_op jit(solution)/shard_map/gather | solution.py:34
  101.1 2.8 %fusion.2 = bf16[4,512,256]{1,2,0:T(8,128)(2,1)S(1)} fusion(bf16[512,896,1]{1,0,2:T(8,128)(2,1)S(1)} %reshape.267, bf16[4,2,896,256]{3,2,1,0:T(8,128)(2,1)} %gather_fusion), kind=kOutput, calls=%fused_computation.19 | convolution fusion | flops 940048384 | bytes 3801088 | tf_op jit(solution)/shard_map/rd,jdh->jrh/dot_general | solution.py:78
  103.9 17.1 %all_to_all.35 = bf16[4,512,256]{1,2,0:T(8,128)(2,1)S(1)} all-to-all(bf16[4,512,256]{1,2,0:T(8,128)(2,1)S(1)} %fusion.2), channel_id=1, replica_groups=mesh['expert'=128,'tensor'=4] {'tensor'}, dimensions={0} | all-to-all | bytes 2097152 | tf_op jit(solution)/shard_map/all_to_all | solution.py:81
  121.5 16.0 %all_to_all.36 = bf16[4,512,256]{2,1,0:T(8,128)(2,1)S(1)} all-to-all(bf16[4,512,256]{2,1,0:T(8,128)(2,1)S(1)} %broadcast_in_dim.21), channel_id=1, replica_groups=mesh['expert'=128,'tensor'=4] {'tensor'}, dimensions={0} | all-to-all | bytes 2097152 | tf_op jit(solution)/shard_map/all_to_all | solution.py:85
  137.5 2.9 %convert_reduce_fusion = bf16[512,896]{1,0:T(8,128)(2,1)S(1)} fusion(bf16[4,512,256]{2,1,0:T(8,128)(2,1)S(1)} %all_to_all.36, bf16[4,2,896,256]{3,2,1,0:T(8,128)(2,1)} %gather_fusion), kind=kOutput, calls=%fused_computation.13 | convolution fusion | flops 942735360 | bytes 3801088 | tf_op jit(solution)/shard_map/jrh,jdh->jrd/dot_general | solution.py:86
  140.4 1.1 reshape.229
  141.5 15.8 %all-to-all-start.5 = ((bf16[128,4,896]{2,1,0:T(4,128)(2,1)}), bf16[128,4,896]{2,1,0:T(4,128)(2,1)S(1)}, u32[]{:S(2)}, u32[]{:S(2)}) async-start(bf16[128,4,896]{2,1,0:T(4,128)(2,1)} %reshape.229), calls=%async_computation.5 | async-start | bytes 1835008 | tf_op jit(solution)/shard_map/all_to_all | solution.py:91
  157.4 28.5 %all-to-all-done.5 = bf16[128,4,896]{2,1,0:T(4,128)(2,1)S(1)} async-done(((bf16[128,4,896]{2,1,0:T(4,128)(2,1)}), bf16[128,4,896]{2,1,0:T(4,128)(2,1)S(1)}, u32[]{:S(2)}, u32[]{:S(2)}) %all-to-all-start.5) | async-done | bytes 917536 | tf_op jit(solution)/shard_map/all_to_all | solution.py:91
  186.2 1.2 gather_fusion.2
  187.8 9.1 %all_to_all.37 = bf16[4,32,896]{2,1,0:T(8,128)(2,1)S(1)} all-to-all(bf16[4,32,896]{2,1,0:T(8,128)(2,1)S(1)} %broadcast_in_dim.22), channel_id=1, replica_groups=mesh['expert'=128,'tensor'=4] {'tensor'}, dimensions={0} | all-to-all | bytes 458752 | tf_op jit(solution)/shard_map/all_to_all | solution.py:97
  196.8 0.7 copy.48
  (48 shorter events, 3.7 us)
Async XLA Ops:
  0.0 10.2 %all-to-all-start = ((bf16[4,8,3584]{2,1,0:T(8,128)(2,1)}), bf16[4,8,3584]{2,1,0:T(8,128)(2,1)S(1)}, u32[]{:S(2)}, u32[]{:S(2)}) async-start(bf16[4,8,3584]{2,1,0:T(8,128)(2,1)} %bitcast.86), calls=%async_computation | async-start | bytes 458752 | tf_op jit(solution)/shard_map/all_to_all | solution.py:36
  12.2 8.7 %all-to-all-start.1 = ((bf16[4,16,896]{2,1,0:T(8,128)(2,1)}), bf16[4,16,896]{2,1,0:T(8,128)(2,1)S(1)}, u32[]{:S(2)}, u32[]{:S(2)}) async-start(bf16[4,16,896]{2,1,0:T(8,128)(2,1)} %bitcast.74), calls=%async_computation.1 | async-start | bytes 229376 | tf_op jit(solution)/shard_map/all_to_all | solution.py:54
  24.6 76.2 %all-to-all-start.2 = ((bf16[128,4,896]{2,1,0:T(4,128)(2,1)}), bf16[128,4,896]{2,1,0:T(4,128)(2,1)S(1)}, u32[]{:S(2)}, u32[]{:S(2)}) async-start(bf16[128,4,896]{2,1,0:T(4,128)(2,1)} %broadcast_select_fusion), calls=%async_computation.2 | async-start | bytes 1835008 | tf_op jit(solution)/shard_map/all_to_all | solution.py:74
  48.9 24.5 %collective-permute-start.1 = (bf16[2,896,256]{2,1,0:T(8,128)(2,1)S(1)}, bf16[2,896,256]{2,1,0:T(8,128)(2,1)S(1)}, u32[]{:S(2)}, u32[]{:S(2)}) collective-permute-start(bf16[2,896,256]{2,1,0:T(8,128)(2,1)S(1)} %get-tuple-element.9), channel_id=1, source_target_pairs={{0,2},{1,3},{2,0},{3,1},{4,6},{5,7},{6,4},{7,5},{8,10},{9,11},{10,... | collective-permute-start | bytes 2752520 | tf_op jit(solution)/shard_map/ppermute | solution.py:32
  51.4 40.3 %collective-permute-start.2 = (bf16[2,896,256]{2,1,0:T(8,128)(2,1)S(1)}, bf16[2,896,256]{2,1,0:T(8,128)(2,1)S(1)}, u32[]{:S(2)}, u32[]{:S(2)}) collective-permute-start(bf16[2,896,256]{2,1,0:T(8,128)(2,1)S(1)} %get-tuple-element.10), channel_id=1, source_target_pairs={{0,3},{1,0},{2,1},{3,2},{4,7},{5,4},{6,5},{7,6},{8,11},{9,8},{10,9... | collective-permute-start | bytes 2752520 | tf_op jit(solution)/shard_map/ppermute | solution.py:32
  55.4 38.8 %collective-permute-start = (bf16[2,896,256]{2,1,0:T(8,128)(2,1)S(1)}, bf16[2,896,256]{2,1,0:T(8,128)(2,1)S(1)}, u32[]{:S(2)}, u32[]{:S(2)}) collective-permute-start(bf16[2,896,256]{2,1,0:T(8,128)(2,1)S(1)} %get-tuple-element.8), channel_id=1, source_target_pairs={{0,1},{1,2},{2,3},{3,0},{4,5},{5,6},{6,7},{7,4},{8,9},{9,10},{10,1... | collective-permute-start | bytes 2752520 | tf_op jit(solution)/shard_map/ppermute | solution.py:32
  137.5 19.9 %copy-start = (f32[32,8]{0,1:T(8,128)S(1)}, f32[32,8]{0,1:T(8,128)}, u32[]{:S(2)}) copy-start(f32[32,8]{0,1:T(8,128)} %param.13) | copy-start | bytes 3076
  141.5 44.4 %all-to-all-start.5 = ((bf16[128,4,896]{2,1,0:T(4,128)(2,1)}), bf16[128,4,896]{2,1,0:T(4,128)(2,1)S(1)}, u32[]{:S(2)}, u32[]{:S(2)}) async-start(bf16[128,4,896]{2,1,0:T(4,128)(2,1)} %reshape.229), calls=%async_computation.5 | async-start | bytes 1835008 | tf_op jit(solution)/shard_map/all_to_all | solution.py:91

commit v6 on v5

--- a/solution.py
+++ b/solution.py
@@ -20,22 +20,24 @@
     tensor_count = lax.axis_size("tensor")
     slot_count = capacity(group_tokens, top_count, expert_count)
     block_count = model_width // QB
-    w_stack = jnp.stack([w_in[0], w_out[0].T])
     width_quarter = model_width // tensor_count
     own = lax.axis_index("tensor")
-    pieces = [lax.dynamic_slice_in_dim(w_stack, own * width_quarter, width_quarter, axis=1)]
-    for shift in range(1, tensor_count):
-        chunk = lax.dynamic_slice_in_dim(
-            w_stack, ((own + shift) % tensor_count) * width_quarter, width_quarter, axis=1
-        )
-        ring = [(u, (u + shift) % tensor_count) for u in range(tensor_count)]
-        pieces.append(lax.ppermute(chunk, "tensor", ring))
-    by_shift = jnp.stack(pieces)
-    w_blocks = by_shift[(own - jnp.arange(tensor_count)) % tensor_count]
 
-    head_terms = lax.all_to_all(
-        attn_partial[0].reshape(tensor_count, -1, model_width), "tensor", split_axis=0, concat_axis=0
-    )
+    def swap(weights, axis):
+        pieces = [lax.dynamic_slice_in_dim(weights, own * width_quarter, width_quarter, axis=axis)]
+        for shift in range(1, tensor_count):
+            start = ((own + shift) % tensor_count) * width_quarter
+            chunk = lax.dynamic_slice_in_dim(weights, start, width_quarter, axis=axis)
+            ring = [(u, (u + shift) % tensor_count) for u in range(tensor_count)]
+            pieces.append(lax.ppermute(chunk, "tensor", ring))
+        by_shift = jnp.stack(pieces)
+        return by_shift[(own - jnp.arange(tensor_count)) % tensor_count]
+
+    w_in_blocks = swap(w_in[0], 0)
+    w_out_blocks = swap(w_out[0], 1)
+
+    head_blocks = attn_partial[0].reshape(tensor_count, -1, model_width)
+    head_terms = lax.all_to_all(head_blocks, "tensor", split_axis=0, concat_axis=0)
     attention = jnp.sum(head_terms.astype(jnp.float32), axis=0)
     residual = (residual_in.astype(jnp.float32) + attention).astype(jnp.bfloat16)
     stream = residual.astype(jnp.float32)
@@ -68,15 +70,14 @@
         .set(jnp.arange(pair_total, dtype=jnp.int32))
     )
     slot_table = slot_table.reshape(expert_count, slot_count)
-    filled = slot_table >= 0
     token_ids = jnp.maximum(slot_table, 0) // top_count
-    row_block = jnp.where(filled[:, :, None], group_input[token_ids], jnp.zeros((), jnp.bfloat16))
+    row_block = group_input[token_ids]
     recv_rows = lax.all_to_all(row_block, "expert", split_axis=0, concat_axis=0, tiled=True)
     sources = recv_rows.shape[0]
     quarter = recv_rows.shape[2]
     rows = recv_rows.reshape(sources * slot_count, quarter)
     pre_blocks = jnp.einsum(
-        "rd,jdh->jrh", rows, w_blocks[:, 0], preferred_element_type=jnp.float32
+        "rd,jdh->jrh", rows, w_in_blocks, preferred_element_type=jnp.float32
     ).astype(jnp.bfloat16)
     pre_terms = lax.all_to_all(pre_blocks, "tensor", split_axis=0, concat_axis=0)
     pre_value = jnp.sum(pre_terms.astype(jnp.float32), axis=0)
@@ -84,7 +85,7 @@
     hidden_copies = jnp.broadcast_to(hidden_part[None], (tensor_count,) + hidden_part.shape)
     hidden_blocks = lax.all_to_all(hidden_copies, "tensor", split_axis=0, concat_axis=0)
     terms = jnp.einsum(
-        "jrh,jdh->jrd", hidden_blocks, w_blocks[:, 1], preferred_element_type=jnp.float32
+        "jrh,jhd->jrd", hidden_blocks, w_out_blocks, preferred_element_type=jnp.float32
     ).astype(jnp.bfloat16)
     summed = jnp.sum(terms.astype(jnp.float32), axis=0)
     expert_out = summed.astype(jnp.bfloat16).reshape(sources, slot_count, quarter)

time: 199 us -> 193 us (0.970)
  blocking collectives: 42.2 us -> 24.3 us
  starting transfers between devices: 52.6 us -> 68.4 us
  other arithmetic: 9.05 us -> 3.55 us
  waiting for transfers between devices: 70.4 us -> 73.9 us
    all_to_all x1 -> x0, blocking collectives: 16 us -> none  [layer(): lax.all_to_all(hidden_copies, 'tensor', split_axis=0, concat_axis=0)]
    ppermute x3 -> x6, starting transfers between devices: 8.41 us -> 18.5 us  [swap(): pieces.append(lax.ppermute(chunk, 'tensor', ring))]
    all_to_all x1 -> x2, starting transfers between devices: 4.83 us -> 8.48 us  [the longest x1 4.96 us: layer(): lax.all_to_all(head_blocks, 'tensor', split_axis=0, concat_axis=0)]
    another operation x5, other arithmetic: 3.98 us -> 0.76 us  [the longest x2 0.5 us: swap(): by_shift = jnp.stack(pieces)]
    unnamed x6 -> x11, local copies, waits for them, and re-layouts: 3.74 us -> 0.86 us
    ppermute x3 -> x6, waiting for transfers between devices: 36.9 us -> 39.3 us  [swap(): pieces.append(lax.ppermute(chunk, 'tensor', ring))]
    gather x3 -> x4, local copies, waits for them, and re-layouts: 6.87 us -> 7.12 us  [the longest x2 3.93 us: swap(): return by_shift[(own - jnp.arange(tensor_count)) % tensor_count]]
  transfers between devices with their start and end apart: 7 -> 11, of which waited for: 6 -> 10; matrix products, arithmetic and copies ran while one was open for 8% -> 5% of each run, Pallas kernels for 0% -> 0%
where the time goes in v6:
time: 193 us; the launch traced here: 192 us
  waiting for transfers between devices  73.9 us (38%)
  starting transfers between devices  68.4 us (35%)
  blocking collectives  24.3 us (13%)
  local copies, waits for them, and re-layouts  15.8 us (8%)
  matrix products  5.62 us (3%)
  other arithmetic  3.55 us (2%)
    ppermute x6, waiting for transfers between devices, swap(): pieces.append(lax.ppermute(chunk, 'tensor', ring))  39.3 us
    all_to_all x1, waiting for transfers between devices, layer(): lax.all_to_all(expert_out, 'expert', split_axis=0, concat_axis=0, tiled=T...  28.5 us
    all_to_all x1, starting transfers between devices, layer(): lax.all_to_all(row_block, 'expert', split_axis=0, concat_axis=0, tiled=True)  19.8 us
    ppermute x6, starting transfers between devices, swap(): pieces.append(lax.ppermute(chunk, 'tensor', ring))  18.5 us
    all_to_all x1, starting transfers between devices, layer(): lax.all_to_all(expert_out, 'expert', split_axis=0, concat_axis=0, tiled=T...  17.8 us
    all_to_all x1, blocking collectives, layer(): lax.all_to_all(pre_blocks, 'tensor', split_axis=0, concat_axis=0)  15.2 us
    all_to_all x1, blocking collectives, layer(): lax.all_to_all(out_copies, 'tensor', split_axis=0, concat_axis=0)  9.08 us
    all_to_all x1, starting transfers between devices, layer(): lax.all_to_all(head_blocks, 'tensor', split_axis=0, concat_axis=0)  4.96 us
  transfers between devices with their start and end apart: 11, of which 10 were waited for; matrix products, arithmetic and copies ran while one was open for 5% of the time, Pallas kernels for 0%

profile of v6, /device:TPU:1, one launch (start us, length us, event | category | flops | bytes accessed | tf_op | source)
XLA Modules:
  0.0 191.9 jit_solution(7755857505060847279)
XLA Ops:
  0.0 5.0 %all-to-all-start = ((bf16[4,8,3584]{2,1,0:T(8,128)(2,1)}), bf16[4,8,3584]{2,1,0:T(8,128)(2,1)S(1)}, u32[]{:S(2)}, u32[]{:S(2)}) async-start(bf16[4,8,3584]{2,1,0:T(8,128)(2,1)} %bitcast.85), calls=%async_computation | async-start | bytes 458752 | tf_op jit(solution)/shard_map/all_to_all | solution.py:40
  7.4 1.4 scatter_custom_fusion
  11.5 3.8 %all-to-all-start.1 = ((bf16[4,16,896]{2,1,0:T(8,128)(2,1)}), bf16[4,16,896]{2,1,0:T(8,128)(2,1)S(1)}, u32[]{:S(2)}, u32[]{:S(2)}) async-start(bf16[4,16,896]{2,1,0:T(8,128)(2,1)} %bitcast.71), calls=%async_computation.1 | async-start | bytes 229376 | tf_op jit(solution)/shard_map/all_to_all | solution.py:56
  15.4 4.7 %all-to-all-done.1 = bf16[4,16,896]{2,1,0:T(8,128)(2,1)S(1)} async-done(((bf16[4,16,896]{2,1,0:T(8,128)(2,1)}), bf16[4,16,896]{2,1,0:T(8,128)(2,1)S(1)}, u32[]{:S(2)}, u32[]{:S(2)}) %all-to-all-start.1) | async-done | bytes 114720 | tf_op jit(solution)/shard_map/all_to_all | solution.py:56
  20.1 2.0 %gather_fusion.1 = bf16[512,896]{1,0:T(8,128)(2,1)S(1)} fusion(bf16[32,896]{1,0:T(8,128)(2,1)S(1)} %slice_bitcast_fusion, s32[1024]{0:T(1024)S(1)} %pad_clamp_fusion.1), kind=kCustom, calls=%fused_computation.1 | custom fusion | bytes 1837056 | tf_op jit(solution)/shard_map/gather | solution.py:74
  22.1 1.1 reshape.246
  23.3 19.8 %all-to-all-start.2 = ((bf16[128,4,896]{2,1,0:T(4,128)(2,1)}), bf16[128,4,896]{2,1,0:T(4,128)(2,1)S(1)}, u32[]{:S(2)}, u32[]{:S(2)}) async-start(bf16[128,4,896]{2,1,0:T(4,128)(2,1)} %reshape.246), calls=%async_computation.2 | async-start | bytes 1835008 | tf_op jit(solution)/shard_map/all_to_all | solution.py:75
  43.3 2.8 %collective-permute-start.2 = (bf16[896,256]{1,0:T(8,128)(2,1)S(1)}, bf16[896,256]{1,0:T(8,128)(2,1)S(1)}, u32[]{:S(2)}, u32[]{:S(2)}) collective-permute-start(bf16[896,256]{1,0:T(8,128)(2,1)S(1)} %get-tuple-element.13), channel_id=1, source_target_pairs={{0,3},{1,0},{2,1},{3,2},{4,7},{5,4},{6,5},{7,6},{8,11},{9,8},{10,9... | collective-permute-start | bytes 1376264 | tf_op jit(solution)/shard_map/ppermute | solution.py:32
  46.1 2.5 %collective-permute-start = (bf16[896,256]{1,0:T(8,128)(2,1)S(1)}, bf16[896,256]{1,0:T(8,128)(2,1)S(1)}, u32[]{:S(2)}, u32[]{:S(2)}) collective-permute-start(bf16[896,256]{1,0:T(8,128)(2,1)S(1)} %get-tuple-element.12), channel_id=1, source_target_pairs={{0,1},{1,2},{2,3},{3,0},{4,5},{5,6},{6,7},{7,4},{8,9},{9,10},{10,1... | collective-permute-start | bytes 1376264 | tf_op jit(solution)/shard_map/ppermute | solution.py:32
  48.6 2.5 %collective-permute-start.1 = (bf16[896,256]{1,0:T(8,128)(2,1)S(1)}, bf16[896,256]{1,0:T(8,128)(2,1)S(1)}, u32[]{:S(2)}, u32[]{:S(2)}) collective-permute-start(bf16[896,256]{1,0:T(8,128)(2,1)S(1)} %get-tuple-element.14), channel_id=1, source_target_pairs={{0,2},{1,3},{2,0},{3,1},{4,6},{5,7},{6,4},{7,5},{8,10},{9,11},{10,... | collective-permute-start | bytes 1376264 | tf_op jit(solution)/shard_map/ppermute | solution.py:32
  51.1 5.2 %collective-permute-done.2 = bf16[896,256]{1,0:T(8,128)(2,1)S(1)} collective-permute-done((bf16[896,256]{1,0:T(8,128)(2,1)S(1)}, bf16[896,256]{1,0:T(8,128)(2,1)S(1)}, u32[]{:S(2)}, u32[]{:S(2)}) %collective-permute-start.2) | collective-permute-done | bytes 458784 | tf_op jit(solution)/shard_map/ppermute | solution.py:32
  56.3 5.2 %collective-permute-done = bf16[896,256]{1,0:T(8,128)(2,1)S(1)} collective-permute-done((bf16[896,256]{1,0:T(8,128)(2,1)S(1)}, bf16[896,256]{1,0:T(8,128)(2,1)S(1)}, u32[]{:S(2)}, u32[]{:S(2)}) %collective-permute-start) | collective-permute-done | bytes 458784 | tf_op jit(solution)/shard_map/ppermute | solution.py:32
  61.5 7.0 %collective-permute-done.1 = bf16[896,256]{1,0:T(8,128)(2,1)S(1)} collective-permute-done((bf16[896,256]{1,0:T(8,128)(2,1)S(1)}, bf16[896,256]{1,0:T(8,128)(2,1)S(1)}, u32[]{:S(2)}, u32[]{:S(2)}) %collective-permute-start.1) | collective-permute-done | bytes 458784 | tf_op jit(solution)/shard_map/ppermute | solution.py:32
  68.7 1.9 gather_fusion
  70.7 1.0 all-to-all-done.2
  71.9 2.8 %fusion = bf16[4,512,256]{1,2,0:T(8,128)(2,1)S(1)} fusion(bf16[4,896,256]{2,1,0:T(8,128)(2,1)} %gather_fusion, bf16[512,896,1]{1,0,2:T(8,128)(2,1)S(1)} %reshape.278), kind=kOutput, calls=%fused_computation.10 | convolution fusion | flops 940048384 | bytes 3801088 | tf_op jit(solution)/shard_map/rd,jdh->jrh/dot_general | solution.py:79
  74.7 15.2 %all_to_all.35 = bf16[4,512,256]{1,2,0:T(8,128)(2,1)S(1)} all-to-all(bf16[4,512,256]{1,2,0:T(8,128)(2,1)S(1)} %fusion), channel_id=1, replica_groups=mesh['expert'=128,'tensor'=4] {'tensor'}, dimensions={0} | all-to-all | bytes 2097152 | tf_op jit(solution)/shard_map/all_to_all | solution.py:82
  90.3 1.1 broadcast_in_dim.7
  91.4 3.5 %all-to-all-start.4 = ((bf16[4,512,256]{2,1,0:T(8,128)(2,1)}), bf16[4,512,256]{2,1,0:T(8,128)(2,1)S(1)}, u32[]{:S(2)}, u32[]{:S(2)}) async-start(bf16[4,512,256]{2,1,0:T(8,128)(2,1)} %broadcast_in_dim.7), calls=%async_computation.4 | async-start | bytes 2097152 | tf_op jit(solution)/shard_map/all_to_all | solution.py:86
  95.1 3.3 %collective-permute-start.3 = (bf16[256,896]{1,0:T(8,128)(2,1)S(1)}, bf16[256,896]{1,0:T(8,128)(2,1)S(1)}, u32[]{:S(2)}, u32[]{:S(2)}) collective-permute-start(bf16[256,896]{1,0:T(8,128)(2,1)S(1)} %get-tuple-element.8), channel_id=1, source_target_pairs={{0,1},{1,2},{2,3},{3,0},{4,5},{5,6},{6,7},{7,4},{8,9},{9,10},{10,1... | collective-permute-start | bytes 1376264 | tf_op jit(solution)/shard_map/ppermute | solution.py:32
  98.4 4.3 %collective-permute-start.4 = (bf16[256,896]{1,0:T(8,128)(2,1)S(1)}, bf16[256,896]{1,0:T(8,128)(2,1)S(1)}, u32[]{:S(2)}, u32[]{:S(2)}) collective-permute-start(bf16[256,896]{1,0:T(8,128)(2,1)S(1)} %get-tuple-element.10), channel_id=1, source_target_pairs={{0,2},{1,3},{2,0},{3,1},{4,6},{5,7},{6,4},{7,5},{8,10},{9,11},{10,... | collective-permute-start | bytes 1376264 | tf_op jit(solution)/shard_map/ppermute | solution.py:32
  102.7 3.1 %collective-permute-start.5 = (bf16[256,896]{1,0:T(8,128)(2,1)S(1)}, bf16[256,896]{1,0:T(8,128)(2,1)S(1)}, u32[]{:S(2)}, u32[]{:S(2)}) collective-permute-start(bf16[256,896]{1,0:T(8,128)(2,1)S(1)} %get-tuple-element.9), channel_id=1, source_target_pairs={{0,3},{1,0},{2,1},{3,2},{4,7},{5,4},{6,5},{7,6},{8,11},{9,8},{10,9... | collective-permute-start | bytes 1376264 | tf_op jit(solution)/shard_map/ppermute | solution.py:32
  105.8 11.3 %collective-permute-done.3 = bf16[256,896]{1,0:T(8,128)(2,1)S(1)} collective-permute-done((bf16[256,896]{1,0:T(8,128)(2,1)S(1)}, bf16[256,896]{1,0:T(8,128)(2,1)S(1)}, u32[]{:S(2)}, u32[]{:S(2)}) %collective-permute-start.3) | collective-permute-done | bytes 458784 | tf_op jit(solution)/shard_map/ppermute | solution.py:32
  117.1 9.4 %collective-permute-done.4 = bf16[256,896]{1,0:T(8,128)(2,1)S(1)} collective-permute-done((bf16[256,896]{1,0:T(8,128)(2,1)S(1)}, bf16[256,896]{1,0:T(8,128)(2,1)S(1)}, u32[]{:S(2)}, u32[]{:S(2)}) %collective-permute-start.4) | collective-permute-done | bytes 458784 | tf_op jit(solution)/shard_map/ppermute | solution.py:32
  126.4 1.2 collective-permute-done.5
  127.9 2.0 %gather_fusion.2 = bf16[4,256,896]{2,1,0:T(8,128)(2,1)} fusion(bf16[4,256,896]{2,1,0:T(8,128)(2,1)S(1)} %pad_maximum_fusion.1, s32[1024]{0:T(1024)S(1)} %pad_clamp_fusion.2), kind=kCustom, calls=%fused_computation.2 | custom fusion | bytes 3670032 | tf_op jit(solution)/shard_map/gather | solution.py:34
  130.0 2.8 %convert_reduce_fusion = bf16[512,896]{1,0:T(8,128)(2,1)S(1)} fusion(bf16[4,512,256]{2,1,0:T(8,128)(2,1)S(1)} %all-to-all-done.4, bf16[4,256,896]{2,1,0:T(8,128)(2,1)} %gather_fusion.2), kind=kOutput, calls=%fused_computation.5 | convolution fusion | flops 942735360 | bytes 3801088 | tf_op jit(solution)/shard_map/jrh,jhd->jrd/dot_general | solution.py:87
  132.8 1.1 reshape.232
  133.9 17.8 %all-to-all-start.5 = ((bf16[128,4,896]{2,1,0:T(4,128)(2,1)}), bf16[128,4,896]{2,1,0:T(4,128)(2,1)S(1)}, u32[]{:S(2)}, u32[]{:S(2)}) async-start(bf16[128,4,896]{2,1,0:T(4,128)(2,1)} %reshape.232), calls=%async_computation.5 | async-start | bytes 1835008 | tf_op jit(solution)/shard_map/all_to_all | solution.py:92
  151.9 28.5 %all-to-all-done.5 = bf16[128,4,896]{2,1,0:T(4,128)(2,1)S(1)} async-done(((bf16[128,4,896]{2,1,0:T(4,128)(2,1)}), bf16[128,4,896]{2,1,0:T(4,128)(2,1)S(1)}, u32[]{:S(2)}, u32[]{:S(2)}) %all-to-all-start.5) | async-done | bytes 917536 | tf_op jit(solution)/shard_map/all_to_all | solution.py:92
  180.6 1.2 gather_fusion.3
  182.2 9.1 %all_to_all.36 = bf16[4,32,896]{2,1,0:T(8,128)(2,1)S(1)} all-to-all(bf16[4,32,896]{2,1,0:T(8,128)(2,1)S(1)} %broadcast_in_dim.8), channel_id=1, replica_groups=mesh['expert'=128,'tensor'=4] {'tensor'}, dimensions={0} | all-to-all | bytes 458752 | tf_op jit(solution)/shard_map/all_to_all | solution.py:98
  (61 shorter events, 7.9 us)
Async XLA Ops:
  0.0 10.4 %copy-start.2 = (bf16[8,3584]{1,0:T(8,128)(2,1)S(1)}, bf16[8,3584]{1,0:T(8,128)(2,1)}, u32[]{:S(2)}) copy-start(bf16[8,3584]{1,0:T(8,128)(2,1)} %param.8) | copy-start | bytes 172036
  0.0 10.3 %all-to-all-start = ((bf16[4,8,3584]{2,1,0:T(8,128)(2,1)}), bf16[4,8,3584]{2,1,0:T(8,128)(2,1)S(1)}, u32[]{:S(2)}, u32[]{:S(2)}) async-start(bf16[4,8,3584]{2,1,0:T(8,128)(2,1)} %bitcast.85), calls=%async_computation | async-start | bytes 458752 | tf_op jit(solution)/shard_map/all_to_all | solution.py:40
  11.5 8.6 %all-to-all-start.1 = ((bf16[4,16,896]{2,1,0:T(8,128)(2,1)}), bf16[4,16,896]{2,1,0:T(8,128)(2,1)S(1)}, u32[]{:S(2)}, u32[]{:S(2)}) async-start(bf16[4,16,896]{2,1,0:T(8,128)(2,1)} %bitcast.71), calls=%async_computation.1 | async-start | bytes 229376 | tf_op jit(solution)/shard_map/all_to_all | solution.py:56
  23.3 19.8 %copy-start = (bf16[1,3584,256]{2,1,0:T(8,128)(2,1)S(1)}, bf16[1,3584,256]{2,1,0:T(8,128)(2,1)}, u32[]{:S(2)}) copy-start(bf16[1,3584,256]{2,1,0:T(8,128)(2,1)} %param.10) | copy-start | bytes 5505028
  23.3 48.4 %all-to-all-start.2 = ((bf16[128,4,896]{2,1,0:T(4,128)(2,1)}), bf16[128,4,896]{2,1,0:T(4,128)(2,1)S(1)}, u32[]{:S(2)}, u32[]{:S(2)}) async-start(bf16[128,4,896]{2,1,0:T(4,128)(2,1)} %reshape.246), calls=%async_computation.2 | async-start | bytes 1835008 | tf_op jit(solution)/shard_map/all_to_all | solution.py:75
  43.3 13.1 %collective-permute-start.2 = (bf16[896,256]{1,0:T(8,128)(2,1)S(1)}, bf16[896,256]{1,0:T(8,128)(2,1)S(1)}, u32[]{:S(2)}, u32[]{:S(2)}) collective-permute-start(bf16[896,256]{1,0:T(8,128)(2,1)S(1)} %get-tuple-element.13), channel_id=1, source_target_pairs={{0,3},{1,0},{2,1},{3,2},{4,7},{5,4},{6,5},{7,6},{8,11},{9,8},{10,9... | collective-permute-start | bytes 1376264 | tf_op jit(solution)/shard_map/ppermute | solution.py:32
  46.1 15.4 %collective-permute-start = (bf16[896,256]{1,0:T(8,128)(2,1)S(1)}, bf16[896,256]{1,0:T(8,128)(2,1)S(1)}, u32[]{:S(2)}, u32[]{:S(2)}) collective-permute-start(bf16[896,256]{1,0:T(8,128)(2,1)S(1)} %get-tuple-element.12), channel_id=1, source_target_pairs={{0,1},{1,2},{2,3},{3,0},{4,5},{5,6},{6,7},{7,4},{8,9},{9,10},{10,1... | collective-permute-start | bytes 1376264 | tf_op jit(solution)/shard_map/ppermute | solution.py:32
  48.6 19.9 %collective-permute-start.1 = (bf16[896,256]{1,0:T(8,128)(2,1)S(1)}, bf16[896,256]{1,0:T(8,128)(2,1)S(1)}, u32[]{:S(2)}, u32[]{:S(2)}) collective-permute-start(bf16[896,256]{1,0:T(8,128)(2,1)S(1)} %get-tuple-element.14), channel_id=1, source_target_pairs={{0,2},{1,3},{2,0},{3,1},{4,6},{5,7},{6,4},{7,5},{8,10},{9,11},{10,... | collective-permute-start | bytes 1376264 | tf_op jit(solution)/shard_map/ppermute | solution.py:32
  90.3 4.6 %copy-start.1 = (bf16[1,256,3584]{2,1,0:T(8,128)(2,1)S(1)}, bf16[1,256,3584]{2,1,0:T(8,128)(2,1)}, u32[]{:S(2)}) copy-start(bf16[1,256,3584]{2,1,0:T(8,128)(2,1)} %param.11) | copy-start | bytes 5505028
  91.4 38.6 %all-to-all-start.4 = ((bf16[4,512,256]{2,1,0:T(8,128)(2,1)}), bf16[4,512,256]{2,1,0:T(8,128)(2,1)S(1)}, u32[]{:S(2)}, u32[]{:S(2)}) async-start(bf16[4,512,256]{2,1,0:T(8,128)(2,1)} %broadcast_in_dim.7), calls=%async_computation.4 | async-start | bytes 2097152 | tf_op jit(solution)/shard_map/all_to_all | solution.py:86
  95.1 22.0 %collective-permute-start.3 = (bf16[256,896]{1,0:T(8,128)(2,1)S(1)}, bf16[256,896]{1,0:T(8,128)(2,1)S(1)}, u32[]{:S(2)}, u32[]{:S(2)}) collective-permute-start(bf16[256,896]{1,0:T(8,128)(2,1)S(1)} %get-tuple-element.8), channel_id=1, source_target_pairs={{0,1},{1,2},{2,3},{3,0},{4,5},{5,6},{6,7},{7,4},{8,9},{9,10},{10,1... | collective-permute-start | bytes 1376264 | tf_op jit(solution)/shard_map/ppermute | solution.py:32
  98.4 28.1 %collective-permute-start.4 = (bf16[256,896]{1,0:T(8,128)(2,1)S(1)}, bf16[256,896]{1,0:T(8,128)(2,1)S(1)}, u32[]{:S(2)}, u32[]{:S(2)}) collective-permute-start(bf16[256,896]{1,0:T(8,128)(2,1)S(1)} %get-tuple-element.10), channel_id=1, source_target_pairs={{0,2},{1,3},{2,0},{3,1},{4,6},{5,7},{6,4},{7,5},{8,10},{9,11},{10,... | collective-permute-start | bytes 1376264 | tf_op jit(solution)/shard_map/ppermute | solution.py:32
  102.7 25.0 %collective-permute-start.5 = (bf16[256,896]{1,0:T(8,128)(2,1)S(1)}, bf16[256,896]{1,0:T(8,128)(2,1)S(1)}, u32[]{:S(2)}, u32[]{:S(2)}) collective-permute-start(bf16[256,896]{1,0:T(8,128)(2,1)S(1)} %get-tuple-element.9), channel_id=1, source_target_pairs={{0,3},{1,0},{2,1},{3,2},{4,7},{5,4},{6,5},{7,6},{8,11},{9,8},{10,9... | collective-permute-start | bytes 1376264 | tf_op jit(solution)/shard_map/ppermute | solution.py:32
  132.8 19.0 %copy-start.3 = (f32[32,8]{0,1:T(8,128)S(1)}, f32[32,8]{0,1:T(8,128)}, u32[]{:S(2)}) copy-start(f32[32,8]{0,1:T(8,128)} %param.13) | copy-start | bytes 3076
  133.9 46.4 %all-to-all-start.5 = ((bf16[128,4,896]{2,1,0:T(4,128)(2,1)}), bf16[128,4,896]{2,1,0:T(4,128)(2,1)S(1)}, u32[]{:S(2)}, u32[]{:S(2)}) async-start(bf16[128,4,896]{2,1,0:T(4,128)(2,1)} %reshape.232), calls=%async_computation.5 | async-start | bytes 1835008 | tf_op jit(solution)/shard_map/all_to_all | solution.py:92

commit v7 on v5

--- a/solution.py
+++ b/solution.py
@@ -20,14 +20,14 @@
     tensor_count = lax.axis_size("tensor")
     slot_count = capacity(group_tokens, top_count, expert_count)
     block_count = model_width // QB
-    w_stack = jnp.stack([w_in[0], w_out[0].T])
     width_quarter = model_width // tensor_count
     own = lax.axis_index("tensor")
+
+    w_stack = jnp.stack([w_in[0], w_out[0].T])
     pieces = [lax.dynamic_slice_in_dim(w_stack, own * width_quarter, width_quarter, axis=1)]
     for shift in range(1, tensor_count):
-        chunk = lax.dynamic_slice_in_dim(
-            w_stack, ((own + shift) % tensor_count) * width_quarter, width_quarter, axis=1
-        )
+        start = ((own + shift) % tensor_count) * width_quarter
+        chunk = lax.dynamic_slice_in_dim(w_stack, start, width_quarter, axis=1)
         ring = [(u, (u + shift) % tensor_count) for u in range(tensor_count)]
         pieces.append(lax.ppermute(chunk, "tensor", ring))
     by_shift = jnp.stack(pieces)

time: 199 us -> 199 us (level)
  no operation moved by 1% of the time
where the time goes in v7:
time: 199 us; the launch traced here: 198 us
  waiting for transfers between devices  70.4 us (35%)
  starting transfers between devices  52.6 us (26%)
  blocking collectives  42.2 us (21%)
  local copies, waits for them, and re-layouts  17.3 us (9%)
  other arithmetic  9.05 us (5%)
  matrix products  5.67 us (3%)
    ppermute x3, waiting for transfers between devices, layer(): pieces.append(lax.ppermute(chunk, 'tensor', ring))  36.9 us
    all_to_all x1, waiting for transfers between devices, layer(): lax.all_to_all(expert_out, 'expert', split_axis=0, concat_axis=0, tiled=T...  28.5 us
    all_to_all x1, starting transfers between devices, layer(): lax.all_to_all(row_block, 'expert', split_axis=0, concat_axis=0, tiled=True)  19.6 us
    all_to_all x1, blocking collectives, layer(): lax.all_to_all(pre_blocks, 'tensor', split_axis=0, concat_axis=0)  17.1 us
    all_to_all x1, blocking collectives, layer(): lax.all_to_all(hidden_copies, 'tensor', split_axis=0, concat_axis=0)  16 us
    all_to_all x1, starting transfers between devices, layer(): lax.all_to_all(expert_out, 'expert', split_axis=0, concat_axis=0, tiled=T...  15.8 us
    all_to_all x1, blocking collectives, layer(): lax.all_to_all(out_copies, 'tensor', split_axis=0, concat_axis=0)  9.08 us
    ppermute x3, starting transfers between devices, layer(): pieces.append(lax.ppermute(chunk, 'tensor', ring))  8.41 us
  transfers between devices with their start and end apart: 7, of which 6 were waited for; matrix products, arithmetic and copies ran while one was open for 8% of the time, Pallas kernels for 0%

profile of v7, /device:TPU:1, one launch (start us, length us, event | category | flops | bytes accessed | tf_op | source)
XLA Modules:
  0.0 197.5 jit_solution(7906963207413043869)
XLA Ops:
  0.0 4.8 %all-to-all-start = ((bf16[4,8,3584]{2,1,0:T(8,128)(2,1)}), bf16[4,8,3584]{2,1,0:T(8,128)(2,1)S(1)}, u32[]{:S(2)}, u32[]{:S(2)}) async-start(bf16[4,8,3584]{2,1,0:T(8,128)(2,1)} %bitcast.86), calls=%async_computation | async-start | bytes 458752 | tf_op jit(solution)/shard_map/all_to_all | solution.py:36
  4.8 0.8 copy.37
  5.8 0.7 broadcast_multiply_fusion
  7.3 1.4 scatter_custom_fusion
  8.7 0.7 convert_element_type.96
  10.2 1.0 fusion.13
  11.5 0.7 copy.50
  12.2 4.0 %all-to-all-start.1 = ((bf16[4,16,896]{2,1,0:T(8,128)(2,1)}), bf16[4,16,896]{2,1,0:T(8,128)(2,1)S(1)}, u32[]{:S(2)}, u32[]{:S(2)}) async-start(bf16[4,16,896]{2,1,0:T(8,128)(2,1)} %bitcast.74), calls=%async_computation.1 | async-start | bytes 229376 | tf_op jit(solution)/shard_map/all_to_all | solution.py:54
  16.2 4.7 %all-to-all-done.1 = bf16[4,16,896]{2,1,0:T(8,128)(2,1)S(1)} async-done(((bf16[4,16,896]{2,1,0:T(8,128)(2,1)}), bf16[4,16,896]{2,1,0:T(8,128)(2,1)S(1)}, u32[]{:S(2)}, u32[]{:S(2)}) %all-to-all-start.1) | async-done | bytes 114720 | tf_op jit(solution)/shard_map/all_to_all | solution.py:54
  20.9 2.0 %gather_fusion.1 = bf16[512,896]{1,0:T(8,128)(2,1)S(1)} fusion(bf16[32,896]{1,0:T(8,128)(2,1)S(1)} %slice_bitcast_fusion.8, s32[1024]{0:T(1024)S(1)} %pad_clamp_fusion.1), kind=kCustom, calls=%fused_computation.1 | custom fusion | bytes 1837056 | tf_op jit(solution)/shard_map/gather | solution.py:73
  23.2 1.5 broadcast_select_fusion
  24.6 19.6 %all-to-all-start.2 = ((bf16[128,4,896]{2,1,0:T(4,128)(2,1)}), bf16[128,4,896]{2,1,0:T(4,128)(2,1)S(1)}, u32[]{:S(2)}, u32[]{:S(2)}) async-start(bf16[128,4,896]{2,1,0:T(4,128)(2,1)} %broadcast_select_fusion), calls=%async_computation.2 | async-start | bytes 1835008 | tf_op jit(solution)/shard_map/all_to_all | solution.py:74
  44.3 2.9 %copy.34 = bf16[1,256,3584]{1,2,0:T(8,128)(2,1)S(1)} copy(bf16[1,256,3584]{2,1,0:T(8,128)(2,1)} %param.11) | data formatting | bytes 3670016 | tf_op args[4]
  47.2 1.7 fusion.5
  48.9 2.5 %collective-permute-start.1 = (bf16[2,896,256]{2,1,0:T(8,128)(2,1)S(1)}, bf16[2,896,256]{2,1,0:T(8,128)(2,1)S(1)}, u32[]{:S(2)}, u32[]{:S(2)}) collective-permute-start(bf16[2,896,256]{2,1,0:T(8,128)(2,1)S(1)} %get-tuple-element.9), channel_id=1, source_target_pairs={{0,2},{1,3},{2,0},{3,1},{4,6},{5,7},{6,4},{7,5},{8,10},{9,11},{10,... | collective-permute-start | bytes 2752520 | tf_op jit(solution)/shard_map/ppermute | solution.py:32
  51.4 4.0 %collective-permute-start.2 = (bf16[2,896,256]{2,1,0:T(8,128)(2,1)S(1)}, bf16[2,896,256]{2,1,0:T(8,128)(2,1)S(1)}, u32[]{:S(2)}, u32[]{:S(2)}) collective-permute-start(bf16[2,896,256]{2,1,0:T(8,128)(2,1)S(1)} %get-tuple-element.10), channel_id=1, source_target_pairs={{0,3},{1,0},{2,1},{3,2},{4,7},{5,4},{6,5},{7,6},{8,11},{9,8},{10,9... | collective-permute-start | bytes 2752520 | tf_op jit(solution)/shard_map/ppermute | solution.py:32
  55.4 1.9 collective-permute-start
  57.3 16.0 %collective-permute-done.1 = bf16[2,896,256]{2,1,0:T(8,128)(2,1)S(1)} collective-permute-done((bf16[2,896,256]{2,1,0:T(8,128)(2,1)S(1)}, bf16[2,896,256]{2,1,0:T(8,128)(2,1)S(1)}, u32[]{:S(2)}, u32[]{:S(2)}) %collective-permute-start.1) | collective-permute-done | bytes 917536 | tf_op jit(solution)/shard_map/ppermute | solution.py:32
  73.3 18.4 %collective-permute-done.2 = bf16[2,896,256]{2,1,0:T(8,128)(2,1)S(1)} collective-permute-done((bf16[2,896,256]{2,1,0:T(8,128)(2,1)S(1)}, bf16[2,896,256]{2,1,0:T(8,128)(2,1)S(1)}, u32[]{:S(2)}, u32[]{:S(2)}) %collective-permute-start.2) | collective-permute-done | bytes 917536 | tf_op jit(solution)/shard_map/ppermute | solution.py:32
  91.7 2.5 %collective-permute-done = bf16[2,896,256]{2,1,0:T(8,128)(2,1)S(1)} collective-permute-done((bf16[2,896,256]{2,1,0:T(8,128)(2,1)S(1)}, bf16[2,896,256]{2,1,0:T(8,128)(2,1)S(1)}, u32[]{:S(2)}, u32[]{:S(2)}) %collective-permute-start) | collective-permute-done | bytes 917536 | tf_op jit(solution)/shard_map/ppermute | solution.py:32
  94.2 2.0 %pad_maximum_fusion = bf16[4,2,896,256]{3,2,1,0:T(8,128)(2,1)} fusion(bf16[1,2,896,256]{3,2,1,0:T(8,128)(2,1)S(1)} %bitcast.80, bf16[1,2,896,256]{3,2,1,0:T(8,128)(2,1)S(1)} %bitcast.79, bf16[1,2,896,256]{3,2,1,0:T(8,128)(2,1)S(1)} %bitcast.81, bf16[1,2,896,256]{3,2,1,0:T(8,128)(2,1)S(1)} %get-tuple-element.7), kind=kLoop, calls=%fused_computation.12 | loop fusion | flops 5505024 | bytes 7340032 | tf_op jit(solution)/shard_map/stack | solution.py:33
  96.2 4.6 %gather_fusion = bf16[4,2,896,256]{3,2,1,0:T(8,128)(2,1)} fusion(bf16[4,2,896,256]{3,2,1,0:T(8,128)(2,1)} %pad_maximum_fusion, s32[1024]{0:T(1024)S(1)} %pad_clamp_fusion.2), kind=kCustom, calls=%fused_computation | custom fusion | bytes 7340048 | tf_op jit(solution)/shard_map/gather | solution.py:34
  101.1 2.8 %fusion.2 = bf16[4,512,256]{1,2,0:T(8,128)(2,1)S(1)} fusion(bf16[512,896,1]{1,0,2:T(8,128)(2,1)S(1)} %reshape.267, bf16[4,2,896,256]{3,2,1,0:T(8,128)(2,1)} %gather_fusion), kind=kOutput, calls=%fused_computation.19 | convolution fusion | flops 940048384 | bytes 3801088 | tf_op jit(solution)/shard_map/rd,jdh->jrh/dot_general | solution.py:78
  103.9 17.1 %all_to_all.35 = bf16[4,512,256]{1,2,0:T(8,128)(2,1)S(1)} all-to-all(bf16[4,512,256]{1,2,0:T(8,128)(2,1)S(1)} %fusion.2), channel_id=1, replica_groups=mesh['expert'=128,'tensor'=4] {'tensor'}, dimensions={0} | all-to-all | bytes 2097152 | tf_op jit(solution)/shard_map/all_to_all | solution.py:81
  121.5 16.0 %all_to_all.36 = bf16[4,512,256]{2,1,0:T(8,128)(2,1)S(1)} all-to-all(bf16[4,512,256]{2,1,0:T(8,128)(2,1)S(1)} %broadcast_in_dim.21), channel_id=1, replica_groups=mesh['expert'=128,'tensor'=4] {'tensor'}, dimensions={0} | all-to-all | bytes 2097152 | tf_op jit(solution)/shard_map/all_to_all | solution.py:85
  137.5 2.9 %convert_reduce_fusion = bf16[512,896]{1,0:T(8,128)(2,1)S(1)} fusion(bf16[4,512,256]{2,1,0:T(8,128)(2,1)S(1)} %all_to_all.36, bf16[4,2,896,256]{3,2,1,0:T(8,128)(2,1)} %gather_fusion), kind=kOutput, calls=%fused_computation.13 | convolution fusion | flops 942735360 | bytes 3801088 | tf_op jit(solution)/shard_map/jrh,jdh->jrd/dot_general | solution.py:86
  140.4 1.1 reshape.229
  141.5 15.8 %all-to-all-start.5 = ((bf16[128,4,896]{2,1,0:T(4,128)(2,1)}), bf16[128,4,896]{2,1,0:T(4,128)(2,1)S(1)}, u32[]{:S(2)}, u32[]{:S(2)}) async-start(bf16[128,4,896]{2,1,0:T(4,128)(2,1)} %reshape.229), calls=%async_computation.5 | async-start | bytes 1835008 | tf_op jit(solution)/shard_map/all_to_all | solution.py:91
  157.4 28.5 %all-to-all-done.5 = bf16[128,4,896]{2,1,0:T(4,128)(2,1)S(1)} async-done(((bf16[128,4,896]{2,1,0:T(4,128)(2,1)}), bf16[128,4,896]{2,1,0:T(4,128)(2,1)S(1)}, u32[]{:S(2)}, u32[]{:S(2)}) %all-to-all-start.5) | async-done | bytes 917536 | tf_op jit(solution)/shard_map/all_to_all | solution.py:91
  186.2 1.2 gather_fusion.2
  187.8 9.1 %all_to_all.37 = bf16[4,32,896]{2,1,0:T(8,128)(2,1)S(1)} all-to-all(bf16[4,32,896]{2,1,0:T(8,128)(2,1)S(1)} %broadcast_in_dim.22), channel_id=1, replica_groups=mesh['expert'=128,'tensor'=4] {'tensor'}, dimensions={0} | all-to-all | bytes 458752 | tf_op jit(solution)/shard_map/all_to_all | solution.py:97
  196.8 0.7 copy.48
  (48 shorter events, 3.7 us)
Async XLA Ops:
  0.0 10.2 %all-to-all-start = ((bf16[4,8,3584]{2,1,0:T(8,128)(2,1)}), bf16[4,8,3584]{2,1,0:T(8,128)(2,1)S(1)}, u32[]{:S(2)}, u32[]{:S(2)}) async-start(bf16[4,8,3584]{2,1,0:T(8,128)(2,1)} %bitcast.86), calls=%async_computation | async-start | bytes 458752 | tf_op jit(solution)/shard_map/all_to_all | solution.py:36
  12.2 8.7 %all-to-all-start.1 = ((bf16[4,16,896]{2,1,0:T(8,128)(2,1)}), bf16[4,16,896]{2,1,0:T(8,128)(2,1)S(1)}, u32[]{:S(2)}, u32[]{:S(2)}) async-start(bf16[4,16,896]{2,1,0:T(8,128)(2,1)} %bitcast.74), calls=%async_computation.1 | async-start | bytes 229376 | tf_op jit(solution)/shard_map/all_to_all | solution.py:54
  24.6 76.2 %all-to-all-start.2 = ((bf16[128,4,896]{2,1,0:T(4,128)(2,1)}), bf16[128,4,896]{2,1,0:T(4,128)(2,1)S(1)}, u32[]{:S(2)}, u32[]{:S(2)}) async-start(bf16[128,4,896]{2,1,0:T(4,128)(2,1)} %broadcast_select_fusion), calls=%async_computation.2 | async-start | bytes 1835008 | tf_op jit(solution)/shard_map/all_to_all | solution.py:74
  48.9 24.5 %collective-permute-start.1 = (bf16[2,896,256]{2,1,0:T(8,128)(2,1)S(1)}, bf16[2,896,256]{2,1,0:T(8,128)(2,1)S(1)}, u32[]{:S(2)}, u32[]{:S(2)}) collective-permute-start(bf16[2,896,256]{2,1,0:T(8,128)(2,1)S(1)} %get-tuple-element.9), channel_id=1, source_target_pairs={{0,2},{1,3},{2,0},{3,1},{4,6},{5,7},{6,4},{7,5},{8,10},{9,11},{10,... | collective-permute-start | bytes 2752520 | tf_op jit(solution)/shard_map/ppermute | solution.py:32
  51.4 40.3 %collective-permute-start.2 = (bf16[2,896,256]{2,1,0:T(8,128)(2,1)S(1)}, bf16[2,896,256]{2,1,0:T(8,128)(2,1)S(1)}, u32[]{:S(2)}, u32[]{:S(2)}) collective-permute-start(bf16[2,896,256]{2,1,0:T(8,128)(2,1)S(1)} %get-tuple-element.10), channel_id=1, source_target_pairs={{0,3},{1,0},{2,1},{3,2},{4,7},{5,4},{6,5},{7,6},{8,11},{9,8},{10,9... | collective-permute-start | bytes 2752520 | tf_op jit(solution)/shard_map/ppermute | solution.py:32
  55.4 38.8 %collective-permute-start = (bf16[2,896,256]{2,1,0:T(8,128)(2,1)S(1)}, bf16[2,896,256]{2,1,0:T(8,128)(2,1)S(1)}, u32[]{:S(2)}, u32[]{:S(2)}) collective-permute-start(bf16[2,896,256]{2,1,0:T(8,128)(2,1)S(1)} %get-tuple-element.8), channel_id=1, source_target_pairs={{0,1},{1,2},{2,3},{3,0},{4,5},{5,6},{6,7},{7,4},{8,9},{9,10},{10,1... | collective-permute-start | bytes 2752520 | tf_op jit(solution)/shard_map/ppermute | solution.py:32
  137.5 19.9 %copy-start = (f32[32,8]{0,1:T(8,128)S(1)}, f32[32,8]{0,1:T(8,128)}, u32[]{:S(2)}) copy-start(f32[32,8]{0,1:T(8,128)} %param.13) | copy-start | bytes 3076
  141.5 44.4 %all-to-all-start.5 = ((bf16[128,4,896]{2,1,0:T(4,128)(2,1)}), bf16[128,4,896]{2,1,0:T(4,128)(2,1)S(1)}, u32[]{:S(2)}, u32[]{:S(2)}) async-start(bf16[128,4,896]{2,1,0:T(4,128)(2,1)} %reshape.229), calls=%async_computation.5 | async-start | bytes 1835008 | tf_op jit(solution)/shard_map/all_to_all | solution.py:91

commit v8 on v6

--- a/solution.py
+++ b/solution.py
@@ -36,8 +36,9 @@
     w_in_blocks = swap(w_in[0], 0)
     w_out_blocks = swap(w_out[0], 1)
 
-    head_blocks = attn_partial[0].reshape(tensor_count, -1, model_width)
-    head_terms = lax.all_to_all(head_blocks, "tensor", split_axis=0, concat_axis=0)
+    head_terms = lax.all_to_all(
+        attn_partial[0].reshape(tensor_count, -1, model_width), "tensor", split_axis=0, concat_axis=0
+    )
     attention = jnp.sum(head_terms.astype(jnp.float32), axis=0)
     residual = (residual_in.astype(jnp.float32) + attention).astype(jnp.bfloat16)
     stream = residual.astype(jnp.float32)
@@ -71,7 +72,8 @@
     )
     slot_table = slot_table.reshape(expert_count, slot_count)
     token_ids = jnp.maximum(slot_table, 0) // top_count
-    row_block = group_input[token_ids]
+    pick = (token_ids[:, :, None] == jnp.arange(group_tokens)[None, None, :]).astype(jnp.bfloat16)
+    row_block = jnp.einsum("esk,kd->esd", pick, group_input, preferred_element_type=jnp.bfloat16)
     recv_rows = lax.all_to_all(row_block, "expert", split_axis=0, concat_axis=0, tiled=True)
     sources = recv_rows.shape[0]
     quarter = recv_rows.shape[2]

time: 193 us -> 193 us (level)
    gather x2 -> x0, local copies, waits for them, and re-layouts: 3.19 us -> none  [layer(): row_block = group_input[token_ids]]
where the time goes in v8:
time: 193 us; the launch traced here: 192 us
  waiting for transfers between devices  74 us (38%)
  starting transfers between devices  68.4 us (35%)
  blocking collectives  24.8 us (13%)
  local copies, waits for them, and re-layouts  15.1 us (8%)
  matrix products  5.75 us (3%)
  other arithmetic  3.53 us (2%)
    ppermute x6, waiting for transfers between devices, swap(): pieces.append(lax.ppermute(chunk, 'tensor', ring))  39.3 us
    all_to_all x1, waiting for transfers between devices, layer(): lax.all_to_all(expert_out, 'expert', split_axis=0, concat_axis=0, tiled=T...  28.5 us
    all_to_all x1, starting transfers between devices, layer(): lax.all_to_all(row_block, 'expert', split_axis=0, concat_axis=0, tiled=True)  19.8 us
    ppermute x6, starting transfers between devices, swap(): pieces.append(lax.ppermute(chunk, 'tensor', ring))  18.5 us
    all_to_all x1, starting transfers between devices, layer(): lax.all_to_all(expert_out, 'expert', split_axis=0, concat_axis=0, tiled=T...  17.9 us
    all_to_all x1, blocking collectives, layer(): lax.all_to_all(pre_blocks, 'tensor', split_axis=0, concat_axis=0)  15.7 us
    all_to_all x1, blocking collectives, layer(): lax.all_to_all(out_copies, 'tensor', split_axis=0, concat_axis=0)  9.08 us
    all_to_all x1, starting transfers between devices, layer(): lax.all_to_all(attn_partial[0].reshape(tensor_count, -1, model_width), 't...  4.96 us
  transfers between devices with their start and end apart: 11, of which 10 were waited for; matrix products, arithmetic and copies ran while one was open for 5% of the time, Pallas kernels for 0%

profile of v8, /device:TPU:1, one launch (start us, length us, event | category | flops | bytes accessed | tf_op | source)
XLA Modules:
  0.0 192.0 jit_solution(4998889739871302436)
XLA Ops:
  0.0 5.0 %all-to-all-start = ((bf16[4,8,3584]{2,1,0:T(8,128)(2,1)}), bf16[4,8,3584]{2,1,0:T(8,128)(2,1)S(1)}, u32[]{:S(2)}, u32[]{:S(2)}) async-start(bf16[4,8,3584]{2,1,0:T(8,128)(2,1)} %bitcast.86), calls=%async_computation | async-start | bytes 458752 | tf_op jit(solution)/shard_map/all_to_all | solution.py:39
  8.1 1.4 scatter_custom_fusion
  11.5 3.7 %all-to-all-start.1 = ((bf16[4,16,896]{2,1,0:T(8,128)(2,1)}), bf16[4,16,896]{2,1,0:T(8,128)(2,1)S(1)}, u32[]{:S(2)}, u32[]{:S(2)}) async-start(bf16[4,16,896]{2,1,0:T(8,128)(2,1)} %bitcast.72), calls=%async_computation.1 | async-start | bytes 229376 | tf_op jit(solution)/shard_map/all_to_all | solution.py:57
  15.3 4.7 %all-to-all-done.1 = bf16[4,16,896]{2,1,0:T(8,128)(2,1)S(1)} async-done(((bf16[4,16,896]{2,1,0:T(8,128)(2,1)}), bf16[4,16,896]{2,1,0:T(8,128)(2,1)S(1)}, u32[]{:S(2)}, u32[]{:S(2)}) %all-to-all-start.1) | async-done | bytes 114720 | tf_op jit(solution)/shard_map/all_to_all | solution.py:57
  20.4 1.6 copy.39
  22.1 19.8 %all-to-all-start.2 = ((bf16[128,4,896]{2,1,0:T(4,128)(2,1)}), bf16[128,4,896]{2,1,0:T(4,128)(2,1)S(1)}, u32[]{:S(2)}, u32[]{:S(2)}) async-start(bf16[128,4,896]{2,1,0:T(4,128)(2,1)} %copy.39), calls=%async_computation.2 | async-start | bytes 1835008 | tf_op jit(solution)/shard_map/all_to_all | solution.py:77
  42.0 2.8 %collective-permute-start.2 = (bf16[896,256]{1,0:T(8,128)(2,1)S(1)}, bf16[896,256]{1,0:T(8,128)(2,1)S(1)}, u32[]{:S(2)}, u32[]{:S(2)}) collective-permute-start(bf16[896,256]{1,0:T(8,128)(2,1)S(1)} %get-tuple-element.13), channel_id=1, source_target_pairs={{0,3},{1,0},{2,1},{3,2},{4,7},{5,4},{6,5},{7,6},{8,11},{9,8},{10,9... | collective-permute-start | bytes 1376264 | tf_op jit(solution)/shard_map/ppermute | solution.py:32
  44.8 2.5 %collective-permute-start = (bf16[896,256]{1,0:T(8,128)(2,1)S(1)}, bf16[896,256]{1,0:T(8,128)(2,1)S(1)}, u32[]{:S(2)}, u32[]{:S(2)}) collective-permute-start(bf16[896,256]{1,0:T(8,128)(2,1)S(1)} %get-tuple-element.12), channel_id=1, source_target_pairs={{0,1},{1,2},{2,3},{3,0},{4,5},{5,6},{6,7},{7,4},{8,9},{9,10},{10,1... | collective-permute-start | bytes 1376264 | tf_op jit(solution)/shard_map/ppermute | solution.py:32
  47.3 2.5 %collective-permute-start.1 = (bf16[896,256]{1,0:T(8,128)(2,1)S(1)}, bf16[896,256]{1,0:T(8,128)(2,1)S(1)}, u32[]{:S(2)}, u32[]{:S(2)}) collective-permute-start(bf16[896,256]{1,0:T(8,128)(2,1)S(1)} %get-tuple-element.14), channel_id=1, source_target_pairs={{0,2},{1,3},{2,0},{3,1},{4,6},{5,7},{6,4},{7,5},{8,10},{9,11},{10,... | collective-permute-start | bytes 1376264 | tf_op jit(solution)/shard_map/ppermute | solution.py:32
  49.9 5.2 %collective-permute-done.2 = bf16[896,256]{1,0:T(8,128)(2,1)S(1)} collective-permute-done((bf16[896,256]{1,0:T(8,128)(2,1)S(1)}, bf16[896,256]{1,0:T(8,128)(2,1)S(1)}, u32[]{:S(2)}, u32[]{:S(2)}) %collective-permute-start.2) | collective-permute-done | bytes 458784 | tf_op jit(solution)/shard_map/ppermute | solution.py:32
  55.1 5.2 %collective-permute-done = bf16[896,256]{1,0:T(8,128)(2,1)S(1)} collective-permute-done((bf16[896,256]{1,0:T(8,128)(2,1)S(1)}, bf16[896,256]{1,0:T(8,128)(2,1)S(1)}, u32[]{:S(2)}, u32[]{:S(2)}) %collective-permute-start) | collective-permute-done | bytes 458784 | tf_op jit(solution)/shard_map/ppermute | solution.py:32
  60.3 7.0 %collective-permute-done.1 = bf16[896,256]{1,0:T(8,128)(2,1)S(1)} collective-permute-done((bf16[896,256]{1,0:T(8,128)(2,1)S(1)}, bf16[896,256]{1,0:T(8,128)(2,1)S(1)}, u32[]{:S(2)}, u32[]{:S(2)}) %collective-permute-start.1) | collective-permute-done | bytes 458784 | tf_op jit(solution)/shard_map/ppermute | solution.py:32
  67.5 1.9 gather_fusion
  69.4 1.0 all-to-all-done.2
  70.4 1.1 reshape.240
  71.6 2.5 %fusion = bf16[4,512,256]{1,2,0:T(8,128)(2,1)S(1)} fusion(bf16[4,896,256]{2,1,0:T(8,128)(2,1)S(1)} %copy-done.2, bf16[512,896,1]{1,0,2:T(8,128)(2,1)} %reshape.240), kind=kOutput, calls=%fused_computation.9 | convolution fusion | flops 940048384 | bytes 3801088 | tf_op jit(solution)/shard_map/rd,jdh->jrh/dot_general | solution.py:81
  74.0 15.7 %all_to_all.35 = bf16[4,512,256]{1,2,0:T(8,128)(2,1)S(1)} all-to-all(bf16[4,512,256]{1,2,0:T(8,128)(2,1)S(1)} %fusion), channel_id=1, replica_groups=mesh['expert'=128,'tensor'=4] {'tensor'}, dimensions={0} | all-to-all | bytes 2097152 | tf_op jit(solution)/shard_map/all_to_all | solution.py:84
  90.2 1.1 broadcast_in_dim.7
  91.3 3.5 %all-to-all-start.4 = ((bf16[4,512,256]{2,1,0:T(8,128)(2,1)}), bf16[4,512,256]{2,1,0:T(8,128)(2,1)S(1)}, u32[]{:S(2)}, u32[]{:S(2)}) async-start(bf16[4,512,256]{2,1,0:T(8,128)(2,1)} %broadcast_in_dim.7), calls=%async_computation.4 | async-start | bytes 2097152 | tf_op jit(solution)/shard_map/all_to_all | solution.py:88
  95.0 3.3 %collective-permute-start.3 = (bf16[256,896]{1,0:T(8,128)(2,1)S(1)}, bf16[256,896]{1,0:T(8,128)(2,1)S(1)}, u32[]{:S(2)}, u32[]{:S(2)}) collective-permute-start(bf16[256,896]{1,0:T(8,128)(2,1)S(1)} %get-tuple-element.8), channel_id=1, source_target_pairs={{0,1},{1,2},{2,3},{3,0},{4,5},{5,6},{6,7},{7,4},{8,9},{9,10},{10,1... | collective-permute-start | bytes 1376264 | tf_op jit(solution)/shard_map/ppermute | solution.py:32
  98.3 4.3 %collective-permute-start.4 = (bf16[256,896]{1,0:T(8,128)(2,1)S(1)}, bf16[256,896]{1,0:T(8,128)(2,1)S(1)}, u32[]{:S(2)}, u32[]{:S(2)}) collective-permute-start(bf16[256,896]{1,0:T(8,128)(2,1)S(1)} %get-tuple-element.10), channel_id=1, source_target_pairs={{0,2},{1,3},{2,0},{3,1},{4,6},{5,7},{6,4},{7,5},{8,10},{9,11},{10,... | collective-permute-start | bytes 1376264 | tf_op jit(solution)/shard_map/ppermute | solution.py:32
  102.6 3.1 %collective-permute-start.5 = (bf16[256,896]{1,0:T(8,128)(2,1)S(1)}, bf16[256,896]{1,0:T(8,128)(2,1)S(1)}, u32[]{:S(2)}, u32[]{:S(2)}) collective-permute-start(bf16[256,896]{1,0:T(8,128)(2,1)S(1)} %get-tuple-element.9), channel_id=1, source_target_pairs={{0,3},{1,0},{2,1},{3,2},{4,7},{5,4},{6,5},{7,6},{8,11},{9,8},{10,9... | collective-permute-start | bytes 1376264 | tf_op jit(solution)/shard_map/ppermute | solution.py:32
  105.7 11.3 %collective-permute-done.3 = bf16[256,896]{1,0:T(8,128)(2,1)S(1)} collective-permute-done((bf16[256,896]{1,0:T(8,128)(2,1)S(1)}, bf16[256,896]{1,0:T(8,128)(2,1)S(1)}, u32[]{:S(2)}, u32[]{:S(2)}) %collective-permute-start.3) | collective-permute-done | bytes 458784 | tf_op jit(solution)/shard_map/ppermute | solution.py:32
  117.0 9.4 %collective-permute-done.4 = bf16[256,896]{1,0:T(8,128)(2,1)S(1)} collective-permute-done((bf16[256,896]{1,0:T(8,128)(2,1)S(1)}, bf16[256,896]{1,0:T(8,128)(2,1)S(1)}, u32[]{:S(2)}, u32[]{:S(2)}) %collective-permute-start.4) | collective-permute-done | bytes 458784 | tf_op jit(solution)/shard_map/ppermute | solution.py:32
  126.3 1.3 collective-permute-done.5
  127.9 2.0 %gather_fusion.1 = bf16[4,256,896]{2,1,0:T(8,128)(2,1)} fusion(bf16[4,256,896]{2,1,0:T(8,128)(2,1)S(1)} %pad_maximum_fusion.1, s32[1024]{0:T(1024)S(1)} %pad_clamp_fusion.1), kind=kCustom, calls=%fused_computation.1 | custom fusion | bytes 3670032 | tf_op jit(solution)/shard_map/gather | solution.py:34
  129.9 2.8 %convert_reduce_fusion = bf16[512,896]{1,0:T(8,128)(2,1)S(1)} fusion(bf16[4,512,256]{2,1,0:T(8,128)(2,1)S(1)} %all-to-all-done.4, bf16[4,256,896]{2,1,0:T(8,128)(2,1)} %gather_fusion.1), kind=kOutput, calls=%fused_computation.4 | convolution fusion | flops 942735360 | bytes 3801088 | tf_op jit(solution)/shard_map/jrh,jhd->jrd/dot_general | solution.py:89
  132.7 1.1 reshape.202
  133.9 17.9 %all-to-all-start.5 = ((bf16[128,4,896]{2,1,0:T(4,128)(2,1)}), bf16[128,4,896]{2,1,0:T(4,128)(2,1)S(1)}, u32[]{:S(2)}, u32[]{:S(2)}) async-start(bf16[128,4,896]{2,1,0:T(4,128)(2,1)} %reshape.202), calls=%async_computation.5 | async-start | bytes 1835008 | tf_op jit(solution)/shard_map/all_to_all | solution.py:94
  151.9 28.5 %all-to-all-done.5 = bf16[128,4,896]{2,1,0:T(4,128)(2,1)S(1)} async-done(((bf16[128,4,896]{2,1,0:T(4,128)(2,1)}), bf16[128,4,896]{2,1,0:T(4,128)(2,1)S(1)}, u32[]{:S(2)}, u32[]{:S(2)}) %all-to-all-start.5) | async-done | bytes 917536 | tf_op jit(solution)/shard_map/all_to_all | solution.py:94
  180.6 1.2 gather_fusion.2
  182.2 9.1 %all_to_all.36 = bf16[4,32,896]{2,1,0:T(8,128)(2,1)S(1)} all-to-all(bf16[4,32,896]{2,1,0:T(8,128)(2,1)S(1)} %broadcast_in_dim.8), channel_id=1, replica_groups=mesh['expert'=128,'tensor'=4] {'tensor'}, dimensions={0} | all-to-all | bytes 458752 | tf_op jit(solution)/shard_map/all_to_all | solution.py:100
  (61 shorter events, 8.2 us)
Async XLA Ops:
  0.0 10.4 %copy-start.3 = (bf16[8,3584]{1,0:T(8,128)(2,1)S(1)}, bf16[8,3584]{1,0:T(8,128)(2,1)}, u32[]{:S(2)}) copy-start(bf16[8,3584]{1,0:T(8,128)(2,1)} %param.8) | copy-start | bytes 172036
  0.0 10.3 %all-to-all-start = ((bf16[4,8,3584]{2,1,0:T(8,128)(2,1)}), bf16[4,8,3584]{2,1,0:T(8,128)(2,1)S(1)}, u32[]{:S(2)}, u32[]{:S(2)}) async-start(bf16[4,8,3584]{2,1,0:T(8,128)(2,1)} %bitcast.86), calls=%async_computation | async-start | bytes 458752 | tf_op jit(solution)/shard_map/all_to_all | solution.py:39
  11.5 8.4 %all-to-all-start.1 = ((bf16[4,16,896]{2,1,0:T(8,128)(2,1)}), bf16[4,16,896]{2,1,0:T(8,128)(2,1)S(1)}, u32[]{:S(2)}, u32[]{:S(2)}) async-start(bf16[4,16,896]{2,1,0:T(8,128)(2,1)} %bitcast.72), calls=%async_computation.1 | async-start | bytes 229376 | tf_op jit(solution)/shard_map/all_to_all | solution.py:57
  20.4 21.5 %copy-start = (bf16[1,3584,256]{2,1,0:T(8,128)(2,1)S(1)}, bf16[1,3584,256]{2,1,0:T(8,128)(2,1)}, u32[]{:S(2)}) copy-start(bf16[1,3584,256]{2,1,0:T(8,128)(2,1)} %param.10) | copy-start | bytes 5505028
  22.1 48.4 %all-to-all-start.2 = ((bf16[128,4,896]{2,1,0:T(4,128)(2,1)}), bf16[128,4,896]{2,1,0:T(4,128)(2,1)S(1)}, u32[]{:S(2)}, u32[]{:S(2)}) async-start(bf16[128,4,896]{2,1,0:T(4,128)(2,1)} %copy.39), calls=%async_computation.2 | async-start | bytes 1835008 | tf_op jit(solution)/shard_map/all_to_all | solution.py:77
  42.0 13.1 %collective-permute-start.2 = (bf16[896,256]{1,0:T(8,128)(2,1)S(1)}, bf16[896,256]{1,0:T(8,128)(2,1)S(1)}, u32[]{:S(2)}, u32[]{:S(2)}) collective-permute-start(bf16[896,256]{1,0:T(8,128)(2,1)S(1)} %get-tuple-element.13), channel_id=1, source_target_pairs={{0,3},{1,0},{2,1},{3,2},{4,7},{5,4},{6,5},{7,6},{8,11},{9,8},{10,9... | collective-permute-start | bytes 1376264 | tf_op jit(solution)/shard_map/ppermute | solution.py:32
  44.8 15.4 %collective-permute-start = (bf16[896,256]{1,0:T(8,128)(2,1)S(1)}, bf16[896,256]{1,0:T(8,128)(2,1)S(1)}, u32[]{:S(2)}, u32[]{:S(2)}) collective-permute-start(bf16[896,256]{1,0:T(8,128)(2,1)S(1)} %get-tuple-element.12), channel_id=1, source_target_pairs={{0,1},{1,2},{2,3},{3,0},{4,5},{5,6},{6,7},{7,4},{8,9},{9,10},{10,1... | collective-permute-start | bytes 1376264 | tf_op jit(solution)/shard_map/ppermute | solution.py:32
  47.3 19.9 %collective-permute-start.1 = (bf16[896,256]{1,0:T(8,128)(2,1)S(1)}, bf16[896,256]{1,0:T(8,128)(2,1)S(1)}, u32[]{:S(2)}, u32[]{:S(2)}) collective-permute-start(bf16[896,256]{1,0:T(8,128)(2,1)S(1)} %get-tuple-element.14), channel_id=1, source_target_pairs={{0,2},{1,3},{2,0},{3,1},{4,6},{5,7},{6,4},{7,5},{8,10},{9,11},{10,... | collective-permute-start | bytes 1376264 | tf_op jit(solution)/shard_map/ppermute | solution.py:32
  69.4 2.1 %copy-start.2 = (bf16[4,896,256]{2,1,0:T(8,128)(2,1)S(1)}, bf16[4,896,256]{2,1,0:T(8,128)(2,1)}, u32[]{:S(2)}) copy-start(bf16[4,896,256]{2,1,0:T(8,128)(2,1)} %gather_fusion) | copy-start | bytes 5505028
  90.2 4.6 %copy-start.1 = (bf16[1,256,3584]{2,1,0:T(8,128)(2,1)S(1)}, bf16[1,256,3584]{2,1,0:T(8,128)(2,1)}, u32[]{:S(2)}) copy-start(bf16[1,256,3584]{2,1,0:T(8,128)(2,1)} %param.11) | copy-start | bytes 5505028
  91.3 38.6 %all-to-all-start.4 = ((bf16[4,512,256]{2,1,0:T(8,128)(2,1)}), bf16[4,512,256]{2,1,0:T(8,128)(2,1)S(1)}, u32[]{:S(2)}, u32[]{:S(2)}) async-start(bf16[4,512,256]{2,1,0:T(8,128)(2,1)} %broadcast_in_dim.7), calls=%async_computation.4 | async-start | bytes 2097152 | tf_op jit(solution)/shard_map/all_to_all | solution.py:88
  95.0 22.0 %collective-permute-start.3 = (bf16[256,896]{1,0:T(8,128)(2,1)S(1)}, bf16[256,896]{1,0:T(8,128)(2,1)S(1)}, u32[]{:S(2)}, u32[]{:S(2)}) collective-permute-start(bf16[256,896]{1,0:T(8,128)(2,1)S(1)} %get-tuple-element.8), channel_id=1, source_target_pairs={{0,1},{1,2},{2,3},{3,0},{4,5},{5,6},{6,7},{7,4},{8,9},{9,10},{10,1... | collective-permute-start | bytes 1376264 | tf_op jit(solution)/shard_map/ppermute | solution.py:32
  98.3 28.0 %collective-permute-start.4 = (bf16[256,896]{1,0:T(8,128)(2,1)S(1)}, bf16[256,896]{1,0:T(8,128)(2,1)S(1)}, u32[]{:S(2)}, u32[]{:S(2)}) collective-permute-start(bf16[256,896]{1,0:T(8,128)(2,1)S(1)} %get-tuple-element.10), channel_id=1, source_target_pairs={{0,2},{1,3},{2,0},{3,1},{4,6},{5,7},{6,4},{7,5},{8,10},{9,11},{10,... | collective-permute-start | bytes 1376264 | tf_op jit(solution)/shard_map/ppermute | solution.py:32
  102.6 25.0 %collective-permute-start.5 = (bf16[256,896]{1,0:T(8,128)(2,1)S(1)}, bf16[256,896]{1,0:T(8,128)(2,1)S(1)}, u32[]{:S(2)}, u32[]{:S(2)}) collective-permute-start(bf16[256,896]{1,0:T(8,128)(2,1)S(1)} %get-tuple-element.9), channel_id=1, source_target_pairs={{0,3},{1,0},{2,1},{3,2},{4,7},{5,4},{6,5},{7,6},{8,11},{9,8},{10,9... | collective-permute-start | bytes 1376264 | tf_op jit(solution)/shard_map/ppermute | solution.py:32
  132.7 19.1 %copy-start.4 = (f32[32,8]{0,1:T(8,128)S(1)}, f32[32,8]{0,1:T(8,128)}, u32[]{:S(2)}) copy-start(f32[32,8]{0,1:T(8,128)} %param.13) | copy-start | bytes 3076
  133.9 46.5 %all-to-all-start.5 = ((bf16[128,4,896]{2,1,0:T(4,128)(2,1)}), bf16[128,4,896]{2,1,0:T(4,128)(2,1)S(1)}, u32[]{:S(2)}, u32[]{:S(2)}) async-start(bf16[128,4,896]{2,1,0:T(4,128)(2,1)} %reshape.202), calls=%async_computation.5 | async-start | bytes 1835008 | tf_op jit(solution)/shard_map/all_to_all | solution.py:94
